TPU v7x, 256 devices: a whole 4x4x8 slice. The times are simulated.
256 devices in a mesh: gx: 32 (over z, y), gy: 8 (over x, core).
Axes of the slice: x: 4, y: 4, z: 8, core: 2. Of those that a mesh axis runs over, the one named last changes fastest.
Arguments:
- fields: float32 [4, 8, 4096, 1024], P(None, None, 'gx', 'gy'), may hold values from -6 to 6
- shift_x: float32 [8, 4096, 1024], P(None, 'gx', 'gy'), may hold values from -0.5 to 0.5
- shift_y: float32 [8, 4096, 1024], P(None, 'gx', 'gy'), may hold values from -0.5 to 0.5
- block_offset: int32 [256, 8], P(None, 'gy'), may hold values from -23 to 23, as said below
- group_inverse: float32 [8, 4096, 128], P(None, 'gx'), as said below
- lower_coupling: float32 [8, 32], P(None, 'gx'), as said below
- upper_coupling: float32 [8, 32], P(None, 'gx'), as said below
Outputs:
- wind_fields: float32 [2, 8, 4096, 1024], P(None, None, 'gx', 'gy')
- tracers: float32 [2, 8, 4096, 1024], P(None, None, 'gx', 'gy')
Inputs may be any that keep to these rules, and one draw needn't show every extreme that they name: `block_offset`: within each aligned run of 8 x-blocks (the blocks of 128 consecutive columns at one y-block), every block departs from a block in the same run or in one of the two runs before or after it, and that run lies inside the grid; at most 4 blocks of a run depart from any one run, and exactly 4 depart from a run two runs away. `group_inverse`: entries are positive. `lower_coupling`: Negative. `upper_coupling`: Negative.
All inputs are finite; a program needn't handle non-finite values.
Results may differ from a plain program's by a relative error of at most 0.0003.
Values sent between devices are 32-bit elements; how exact they have to be, the bound alone decides.
No kernel may reach another device: no remote copies, remote signals or barrier semaphores. Data moves between devices by JAX's collectives and lax.ppermute only.
A program may use at most 128 MiB of HBM per device.

v0:
```python
import jax
import jax.numpy as jnp
from jax import lax
from jax.sharding import PartitionSpec as P

BX = 16


PRECISE = lax.Precision.HIGHEST


def padded_2(block, sides, width):
    for axis, dim in sides:
        count = lax.axis_size(axis)
        forward = [(i, i + 1) for i in range(count - 1)]
        backward = [(target, source) for source, target in forward]
        low = lax.ppermute(
            lax.slice_in_dim(block, block.shape[dim] - width, None, axis=dim), axis, forward
        )
        high = lax.ppermute(lax.slice_in_dim(block, 0, width, axis=dim), axis, backward)
        block = jnp.concatenate([low, block, high], axis=dim)
    return block


def shifted_2(value, axis, steps):
    count = lax.axis_size(axis)
    leading, last = (max(0, -steps), min(count, count - steps))
    return lax.ppermute(value, axis, [(source, source + steps) for source in range(leading, last)])


def carried_in(value, axis, combine, identity, reverse):
    length, position = (lax.axis_size(axis), lax.axis_index(axis))
    everything = jax.tree.map(lambda part: lax.all_gather(part, axis), value)
    start = jax.tree.map(
        lambda part, zero: jnp.broadcast_to(jnp.asarray(zero, part.dtype), part.shape),
        value,
        identity,
    )

    def hop(k, before):
        at = length - 1 - k if reverse else k
        reached = at > position if reverse else at < position
        new = combine(before, jax.tree.map(lambda part: part[at], everything))
        return jax.tree.map(lambda a, b: jnp.where(reached, a, b), new, before)

    return lax.fori_loop(0, length, hop, start)


def lagrange(displace):
    position = -displace
    weights = []
    for target in range(-2, 3):
        factor = jnp.ones_like(position)
        for anchor in range(-2, 3):
            if anchor != target:
                factor = factor * ((position - anchor) / (target - anchor))
        weights.append(factor)
    return weights


def interpolate(window, across, along, span_x, span_y):
    weights_x = lagrange(across)
    weights_y = lagrange(along)
    running_total = None
    for column_tap in range(5):
        partial_sum = weights_y[0] * window[..., column_tap : column_tap + span_x, 0:span_y]
        for row_tap in range(1, 5):
            partial_sum = (
                partial_sum
                + weights_y[row_tap]
                * window[..., column_tap : column_tap + span_x, row_tap : row_tap + span_y]
            )
        tap_term = weights_x[column_tap] * partial_sum
        running_total = tap_term if running_total is None else running_total + tap_term
    return running_total


def compose(earlier, latter):
    product = jnp.einsum("...ij,...jk->...ik", latter, earlier, precision=PRECISE)
    return product / product[..., 1:2, 1:2]


def chain_affine(earlier, latter):
    return (latter[0] * earlier[0], latter[0][..., None, :, None] * earlier[1] + latter[1])


def mobius(lead_left, tail_left, lead_right, tail_right):
    upper_row = jnp.stack([tail_left * lead_right - tail_right * lead_left, tail_right], axis=-1)
    lower_row = jnp.stack([-lead_left, jnp.ones_like(lead_left)], axis=-1)
    return jnp.stack([upper_row, lower_row], axis=-2)


def local(fields, shift_x, shift_y, block_offset, group_inverse, lower_coupling, upper_coupling):
    field_count, level_count, columns, rows_here = fields.shape
    block_count = columns // BX
    position = lax.axis_index("gx")
    padded = padded_2(fields, (("gx", 2), ("gy", 3)), 2)
    offsets = block_offset[:, 0]
    inside = jnp.arange(block_count, dtype=jnp.int32)
    own_offset = lax.dynamic_slice_in_dim(offsets, position * block_count, block_count)
    shifted = []
    for step_distance in (2, 1, -1, -2):
        shifted.append(shifted_2(padded, "gx", step_distance))
    window_field = jnp.concatenate(
        [
            shifted[0][:, :, 0 : columns + 2],
            shifted[1][:, :, 2 : columns + 2],
            padded[:, :, 2 : columns + 2],
            shifted[2][:, :, 2 : columns + 2],
            shifted[3][:, :, 2 : columns + 4],
        ],
        axis=2,
    )
    starts = (inside - own_offset) * BX + 2 * columns
    windows = jnp.stack(
        [
            lax.dynamic_slice_in_dim(window_field, starts[column_block], BX + 4, 2)
            for column_block in range(block_count)
        ]
    )
    across = shift_x.reshape(level_count, block_count, BX, rows_here).transpose(1, 0, 2, 3)[:, None]
    along = shift_y.reshape(level_count, block_count, BX, rows_here).transpose(1, 0, 2, 3)[:, None]
    interpolated = interpolate(windows, across, along, BX, rows_here)
    advected = interpolated.transpose(1, 2, 0, 3, 4).reshape(
        field_count, level_count, columns, rows_here
    )
    local_solve = jnp.einsum("lij,wljy->wliy", group_inverse, advected[0:2], precision=PRECISE)
    lower_here = lower_coupling[:, 0]
    upper_here = upper_coupling[:, 0]
    left_spike = group_inverse[:, :, 0] * lower_here[:, None]
    right_spike = group_inverse[:, :, columns - 1] * upper_here[:, None]
    lead_left = left_spike[:, 0]
    tail_left = left_spike[:, columns - 1]
    lead_right = right_spike[:, 0]
    tail_right = right_spike[:, columns - 1]
    first_row = local_solve[:, :, 0, :]
    last_row = local_solve[:, :, columns - 1, :]
    identity_map = jnp.broadcast_to(jnp.eye(2, dtype=jnp.float32), (level_count, 2, 2))
    ones_level = jnp.ones((level_count,), jnp.float32)
    zeros_rows = jnp.zeros_like(first_row)
    before = carried_in(
        mobius(lead_left, tail_left, lead_right, tail_right), "gx", compose, identity_map, False
    )
    gain_here = before[:, 0, 1] / before[:, 1, 1]
    pivot_here = 1.0 - lead_left * gain_here
    ratio_here = tail_left * gain_here / pivot_here
    forward_map = (
        -(ratio_here * lead_left + tail_left),
        ratio_here[None, :, None] * first_row + last_row,
    )
    behind = carried_in(forward_map, "gx", chain_affine, (ones_level, zeros_rows), False)[1]
    lead_value = first_row - lead_left[None, :, None] * behind
    backward_map = (-lead_right / pivot_here, lead_value / pivot_here[None, :, None])
    ahead_value = carried_in(backward_map, "gx", chain_affine, (ones_level, zeros_rows), True)[1]
    first_value = backward_map[1] + backward_map[0][None, :, None] * ahead_value
    left_value = behind - gain_here[None, :, None] * first_value
    wind_fields = (
        local_solve
        - left_spike[None, :, :, None] * left_value[:, :, None, :]
        - right_spike[None, :, :, None] * ahead_value[:, :, None, :]
    )
    return (wind_fields, advected[2:4])


def solution(mesh):
    return jax.shard_map(
        local,
        mesh=mesh,
        in_specs=(
            P(None, None, "gx", "gy"),
            P(None, "gx", "gy"),
            P(None, "gx", "gy"),
            P(None, "gy"),
            P(None, "gx", None),
            P(None, "gx"),
            P(None, "gx"),
        ),
        out_specs=(P(None, None, "gx", "gy"), P(None, None, "gx", "gy")),
        check_vma=False,
    )
```

profile of v0, /device:TPU:34, one launch (start us, length us, event | category | flops | bytes accessed | tf_op | source)
XLA Modules:
  0.0 843.2 jit_solution(16945281396783806040)
XLA Ops:
  1.7 3.5 collective-permute-start
  5.2 4.5 collective-permute-start.1
  9.7 1.4 fusion.69
  12.0 2.8 constant_dynamic-update-slice_fusion.1
  14.9 2.6 fusion.66
  17.5 2.8 copy.98
  20.3 1.9 collective-permute-start.2
  22.3 2.8 copy.99
  25.1 3.6 collective-permute-start.3
  28.9 50.9 %all-gather = f32[256,2,2]{2,1,0:T(2,128)S(1)} all-gather(f32[8,2,2]{2,1,0:T(2,128)S(1)} %copy.110), channel_id=2, replica_groups=mesh['gx'=32,'gy'=8] {'gx'}, dimensions={0}, use_global_device_ids=true | all-gather | bytes 4224 | tf_op jit(solution)/shard_map/all_gather | solution.py:33
  80.3 2.6 copy.100
  82.9 2.6 copy.101
  85.5 6.0 pad_maximum_fusion
  91.5 3.5 collective-permute-start.4
  95.0 2.3 collective-permute-start.5
  97.4 20.1 %while.43 = (s32[]{:T(128)}, f32[8,2,2]{2,1,0:T(2,128)S(1)}, s32[]{:T(128)}, f32[32,8,2,2]{1,3,2,0:T(2,128)S(1)}, s32[]{:T(128)}) while((s32[]{:T(128)}, f32[8,2,2]{2,1,0:T(2,128)S(1)}, s32[]{:T(128)}, f32[32,8,2,2]{1,3,2,0:T(2,128)S(1)}, s32[]{:T(128)}) %tuple.142), condition=%wide.region_1.2_spmd, body=%wide.region_0.1_spmd.sunk | while | flops 835 | bytes 1451 | solution.py:46
  134.8 169.4 %all-gather.2 = f32[32,1,8]{2,1,0:T(1,128)} all-gather(f32[1,1,8]{2,1,0:T(1,128)S(1)} %get-tuple-element.460), channel_id=1, replica_groups=mesh['gx'=32,'gy'=8] {'gx'}, dimensions={0}, use_global_device_ids=true | all-gather | bytes 1056 | tf_op jit(solution)/shard_map/all_gather | solution.py:33
  304.2 39.5 %all-gather.3 = f32[32,1,8]{2,1,0:T(1,128)} all-gather(f32[1,1,8]{2,1,0:T(1,128)S(1)} %get-tuple-element.461), channel_id=1, replica_groups=mesh['gx'=32,'gy'=8] {'gx'}, dimensions={0}, use_global_device_ids=true | all-gather | bytes 1056 | tf_op jit(solution)/shard_map/all_gather | solution.py:33
  343.8 3.0 collective-permute-start.6
  347.3 4.2 collective-permute-start.7
  351.5 4.2 fusion.36
  355.7 2.6 slice_dynamic-update-slice_fusion.1
  358.3 2.8 slice_dynamic-update-slice_fusion.4
  361.2 2.8 slice_dynamic-update-slice_fusion.3
  364.0 162.7 %collective-permute-done.6 = f32[4,8,132,132]{3,1,2,0:T(8,128)S(1)} collective-permute-done((f32[4,8,132,132]{3,1,2,0:T(8,128)}, f32[4,8,132,132]{3,1,2,0:T(8,128)S(1)}, u32[]{:S(2)}, u32[]{:S(2)}) %collective-permute-start.6) | collective-permute-done | bytes 2230304 | tf_op jit(solution)/shard_map/ppermute | solution.py:28
  527.3 81.0 %collective-permute-done.7 = f32[4,8,132,132]{3,1,2,0:T(8,128)S(1)} collective-permute-done((f32[4,8,132,132]{3,1,2,0:T(8,128)}, f32[4,8,132,132]{3,1,2,0:T(8,128)S(1)}, u32[]{:S(2)}, u32[]{:S(2)}) %collective-permute-start.7) | collective-permute-done | bytes 2230304 | tf_op jit(solution)/shard_map/ppermute | solution.py:28
  616.3 38.7 %fusion.5 = f32[4,8,8,16,128]{4,1,3,0,2:T(8,128)S(1)} fusion(f32[8,4,8,20,132]{4,2,3,1,0:T(8,128)} %bitcast_dynamic-update-slice_fusion, f32[8,8,16,128]{3,1,2,0:T(8,128)} %get-tuple-element.475, f32[8,8,16,128]{3,1,2,0:T(8,128)} %get-tuple-element.474, f32[8,8,16,128]{3,1,2,0:T(8,128)} %get-tuple-element.472, f32[8,8,16,128]{3,1,2,0:T(8,128)} %get-tuple-element.473, ...), kind=kLoop, calls=%fused_computation.19 | loop fusion | flops 28311552 | bytes 59768832 | tf_op jit(solution)/shard_map/transpose | solution.py:124
  658.0 48.8 %all_gather.27 = f32[32,2,8,128]{3,2,1,0:T(8,128)S(1)} all-gather(f32[1,2,8,128]{3,2,1,0:T(8,128)S(1)} %fusion.52), channel_id=1, replica_groups=mesh['gx'=32,'gy'=8] {'gx'}, dimensions={0}, use_global_device_ids=true | all-gather | bytes 270336 | tf_op jit(solution)/shard_map/all_gather | solution.py:33
  706.8 61.5 %while.44 = (s32[]{:T(128)}, f32[2,8,128]{2,1,0:T(8,128)S(1)}, s32[]{:T(128)}, f32[32,8]{1,0:T(8,128)}, f32[32,2,8,128]{3,2,1,0:T(8,128)S(1)}, /*index=5*/s32[]{:T(128)}, s32[]{:T(128)}) while((s32[]{:T(128)}, f32[2,8,128]{2,1,0:T(8,128)S(1)}, s32[]{:T(128)}, f32[32,8]{1,0:T(8,128)}, f32[32,2,8,128]{3,2,1,0:T(8,128)S(1)}, ...), condition=%wide.region_3.4_spmd.clone, body=%wide.region_2.3_spmd.clone.sunk | while | flops 8196 | bytes 24777 | solution.py:46
  706.8 1.2 dynamic-slice_bitcast_fusion.7
  708.7 1.2 dynamic-slice_bitcast_fusion.7
  710.6 1.2 dynamic-slice_bitcast_fusion.7
  712.5 1.2 dynamic-slice_bitcast_fusion.7
  714.4 1.2 dynamic-slice_bitcast_fusion.7
  716.3 1.2 dynamic-slice_bitcast_fusion.7
  718.3 1.2 dynamic-slice_bitcast_fusion.7
  720.2 1.2 dynamic-slice_bitcast_fusion.7
  722.1 1.2 dynamic-slice_bitcast_fusion.7
  724.0 1.2 dynamic-slice_bitcast_fusion.7
  725.9 1.2 dynamic-slice_bitcast_fusion.7
  727.8 1.2 dynamic-slice_bitcast_fusion.7
  729.8 1.2 dynamic-slice_bitcast_fusion.7
  731.7 1.2 dynamic-slice_bitcast_fusion.7
  733.6 1.2 dynamic-slice_bitcast_fusion.7
  735.5 1.2 dynamic-slice_bitcast_fusion.7
  737.4 1.2 dynamic-slice_bitcast_fusion.7
  739.4 1.2 dynamic-slice_bitcast_fusion.7
  741.3 1.2 dynamic-slice_bitcast_fusion.7
  743.2 1.2 dynamic-slice_bitcast_fusion.7
  745.1 1.2 dynamic-slice_bitcast_fusion.7
  747.1 1.2 dynamic-slice_bitcast_fusion.7
  749.0 1.2 dynamic-slice_bitcast_fusion.7
  750.9 1.2 dynamic-slice_bitcast_fusion.7
  752.8 1.2 dynamic-slice_bitcast_fusion.7
  754.8 1.2 dynamic-slice_bitcast_fusion.7
  756.7 1.2 dynamic-slice_bitcast_fusion.7
  758.6 1.2 dynamic-slice_bitcast_fusion.7
  760.5 1.2 dynamic-slice_bitcast_fusion.7
  762.5 1.2 dynamic-slice_bitcast_fusion.7
  764.4 1.2 dynamic-slice_bitcast_fusion.7
  766.3 1.2 dynamic-slice_bitcast_fusion.7
  768.9 46.2 %all-gather.1 = f32[64,8,128]{2,1,0:T(8,128)S(1)} all-gather(f32[2,8,128]{2,1,0:T(8,128)S(1)} %fusion.53), channel_id=3, replica_groups=mesh['gx'=32,'gy'=8] {'gx'}, dimensions={0}, use_global_device_ids=true | all-gather | bytes 270336 | tf_op jit(solution)/shard_map/all_gather | solution.py:33
  815.1 24.2 %while.45 = (s32[]{:T(128)}, f32[2,8,128]{2,1,0:T(8,128)S(1)}, s32[]{:T(128)}, f32[32,8]{1,0:T(8,128)}, f32[32,2,8,128]{3,2,1,0:T(8,128)S(1)}, /*index=5*/s32[]{:T(128)}, s32[]{:T(128)}, s32[]{:T(128)}, s32[]{:T(128)}) while((s32[]{:T(128)}, f32[2,8,128]{2,1,0:T(8,128)S(1)}, s32[]{:T(128)}, f32[32,8]{1,0:T(8,128)}, ...), condition=%wide.region_5.6_spmd.clone, body=%wide.region_4.5_spmd.clone.sunk | while | flops 8200 | bytes 24839 | solution.py:46
  840.7 1.3 copy.115
  (330 shorter events, 87.2 us)
Async XLA Ops:
  0.6 10.8 %copy-start.7 = (f32[8,1]{0,1:T(1,128)S(1)}, f32[8,1]{0,1:T(1,128)}, u32[]{:S(2)}) copy-start(f32[8,1]{0,1:T(1,128)} %param.18) | copy-start | bytes 100
  0.6 10.8 %copy-start.6 = (f32[8,1]{0,1:T(1,128)S(1)}, f32[8,1]{0,1:T(1,128)}, u32[]{:S(2)}) copy-start(f32[8,1]{0,1:T(1,128)} %param.19) | copy-start | bytes 100
  1.7 10.3 %collective-permute-start = (f32[4,8,2,128]{3,1,2,0:T(8,128)S(1)}, f32[4,8,2,128]{3,1,2,0:T(8,128)S(1)}, u32[]{:S(2)}, u32[]{:S(2)}) collective-permute-start(f32[4,8,2,128]{3,1,2,0:T(8,128)S(1)} %copy.136), channel_id=1, source_target_pairs={{0,8},{8,16},{16,24},{24,32},{32,40},{40,48},{48,56},{56,64},{64,7... | collective-permute-start | bytes 98312 | tf_op jit(solution)/shard_map/ppermute | solution.py:17
  5.2 9.7 %collective-permute-start.1 = (f32[4,8,2,128]{3,1,2,0:T(8,128)S(1)}, f32[4,8,2,128]{3,1,2,0:T(8,128)S(1)}, u32[]{:S(2)}, u32[]{:S(2)}) collective-permute-start(f32[4,8,2,128]{3,1,2,0:T(8,128)S(1)} %copy.137), channel_id=1, source_target_pairs={{8,0},{16,8},{24,16},{32,24},{40,32},{48,40},{56,48},{64,56},{72,6... | collective-permute-start | bytes 98312 | tf_op jit(solution)/shard_map/ppermute | solution.py:20
  11.7 335.1 %copy-start.4 = (f32[8]{0:T(128)}, f32[8]{0:T(128)S(1)}, u32[]{:S(2)}) copy-start(f32[8]{0:T(128)S(1)} %get-tuple-element.407) | copy-start | bytes 100
  20.3 59.9 %collective-permute-start.2 = (f32[4,8,132,2]{2,1,3,0:T(8,128)S(1)}, f32[4,8,132,2]{2,1,3,0:T(8,128)S(1)}, u32[]{:S(2)}, u32[]{:S(2)}) collective-permute-start(f32[4,8,132,2]{2,1,3,0:T(8,128)S(1)} %copy.98), channel_id=1, source_target_pairs={{0,1},{1,2},{2,3},{3,4},{4,5},{5,6},{6,7},{8,9},{9,10},{10,11},{11... | collective-permute-start | bytes 101384 | tf_op jit(solution)/shard_map/ppermute | solution.py:17
  25.1 57.8 %collective-permute-start.3 = (f32[4,8,132,2]{2,1,3,0:T(8,128)S(1)}, f32[4,8,132,2]{2,1,3,0:T(8,128)S(1)}, u32[]{:S(2)}, u32[]{:S(2)}) collective-permute-start(f32[4,8,132,2]{2,1,3,0:T(8,128)S(1)} %copy.99), channel_id=1, source_target_pairs={{1,0},{2,1},{3,2},{4,3},{5,4},{6,5},{7,6},{9,8},{10,9},{11,10},{12... | collective-permute-start | bytes 101384 | tf_op jit(solution)/shard_map/ppermute | solution.py:20
  85.5 32.0 %copy-start.8 = (s32[256,1]{0,1:T(1,128)S(1)}, s32[256,1]{0,1:T(1,128)}, u32[]{:S(2)}) copy-start(s32[256,1]{0,1:T(1,128)} %param.16) | copy-start | bytes 3076
  85.5 42.6 %copy-start.1 = (f32[8,128,128]{2,1,0:T(8,128)S(1)}, f32[8,128,128]{2,1,0:T(8,128)}, u32[]{:S(2)}) copy-start(f32[8,128,128]{2,1,0:T(8,128)} %param.14) | copy-start | bytes 1572868
  91.5 37.4 %copy-start.2 = (f32[8,128,128]{2,1,0:T(8,128)S(1)}, f32[8,128,128]{2,1,0:T(8,128)}, u32[]{:S(2)}) copy-start(f32[8,128,128]{2,1,0:T(8,128)} %param.15) | copy-start | bytes 1572868
  91.5 264.2 %collective-permute-start.4 = (f32[4,8,132,132]{3,1,2,0:T(8,128)}, f32[4,8,132,132]{3,1,2,0:T(8,128)}, u32[]{:S(2)}, u32[]{:S(2)}) collective-permute-start(f32[4,8,132,132]{3,1,2,0:T(8,128)} %pad_maximum_fusion), channel_id=1, source_target_pairs={{0,16},{8,24},{16,32},{24,40},{32,48},{40,56},{48,64},{56,72},{64,... | collective-permute-start | bytes 6690824 | tf_op jit(solution)/shard_map/ppermute | solution.py:28
  95.0 263.3 %collective-permute-start.5 = (f32[4,8,132,132]{3,1,2,0:T(8,128)}, f32[4,8,132,132]{3,1,2,0:T(8,128)}, u32[]{:S(2)}, u32[]{:S(2)}) collective-permute-start(f32[4,8,132,132]{3,1,2,0:T(8,128)} %pad_maximum_fusion), channel_id=1, source_target_pairs={{0,8},{8,16},{16,24},{24,32},{32,40},{40,48},{48,56},{56,64},{64,7... | collective-permute-start | bytes 6690824 | tf_op jit(solution)/shard_map/ppermute | solution.py:28
  134.8 220.9 %copy-start.3 = (f32[8]{0:T(128)}, f32[8]{0:T(128)S(1)}, u32[]{:S(2)}) copy-start(f32[8]{0:T(128)S(1)} %fusion.54) | copy-start | bytes 100
  343.8 182.9 %collective-permute-start.6 = (f32[4,8,132,132]{3,1,2,0:T(8,128)}, f32[4,8,132,132]{3,1,2,0:T(8,128)S(1)}, u32[]{:S(2)}, u32[]{:S(2)}) collective-permute-start(f32[4,8,132,132]{3,1,2,0:T(8,128)} %pad_maximum_fusion), channel_id=1, source_target_pairs={{8,0},{16,8},{24,16},{32,24},{40,32},{48,40},{56,48},{64,56},{72,6... | collective-permute-start | bytes 6690824 | tf_op jit(solution)/shard_map/ppermute | solution.py:28
  347.3 8.4 copy-start.5
  347.3 261.1 %collective-permute-start.7 = (f32[4,8,132,132]{3,1,2,0:T(8,128)}, f32[4,8,132,132]{3,1,2,0:T(8,128)S(1)}, u32[]{:S(2)}, u32[]{:S(2)}) collective-permute-start(f32[4,8,132,132]{3,1,2,0:T(8,128)} %pad_maximum_fusion), channel_id=1, source_target_pairs={{16,0},{24,8},{32,16},{40,24},{48,32},{56,40},{64,48},{72,56},{80,... | collective-permute-start | bytes 6690824 | tf_op jit(solution)/shard_map/ppermute | solution.py:28
  655.2 1.0 copy-start
where the time goes:
time: 849 us; the launch traced here: 843 us
  blocking collectives  355 us (42%)
  waiting for transfers between devices  244 us (29%)
  local copies, waits for them, and re-layouts  112 us (13%)
  other arithmetic  82.8 us (10%)
  starting transfers between devices  26.5 us (3%)
  between operations  15.4 us (2%)
    all_gather x5, blocking collectives, carried_in(): everything = jax.tree.map(lambda part: lax.all_gather(part, axis), value)  355 us
    ppermute x4, waiting for transfers between devices, shifted_2(): lax.ppermute(value, axis, [(source, source + steps) for source in range(l...  244 us
    mul x64, local copies, waits for them, and re-layouts, chain_affine(): latter[0][..., None, :, None] * earlier[1] + latter[1]  60 us
    transpose x1, other arithmetic, local(): interpolated.transpose(1, 2, 0, 3, 4)  38.7 us
    select_n x96, other arithmetic, hop(): return jax.tree.map(lambda a, b: jnp.where(reached, a, b), new, before)  28.9 us
    unnamed x37, local copies, waits for them, and re-layouts  20.6 us
  transfers between devices with their start and end apart: 8, of which 2 were waited for; matrix products, arithmetic and copies ran while one was open for 6% of the time, Pallas kernels for 0%

commit v1 on v0

--- a/solution.py
+++ b/solution.py
@@ -26,24 +26,6 @@
     count = lax.axis_size(axis)
     leading, last = (max(0, -steps), min(count, count - steps))
     return lax.ppermute(value, axis, [(source, source + steps) for source in range(leading, last)])
-
-
-def carried_in(value, axis, combine, identity, reverse):
-    length, position = (lax.axis_size(axis), lax.axis_index(axis))
-    everything = jax.tree.map(lambda part: lax.all_gather(part, axis), value)
-    start = jax.tree.map(
-        lambda part, zero: jnp.broadcast_to(jnp.asarray(zero, part.dtype), part.shape),
-        value,
-        identity,
-    )
-
-    def hop(k, before):
-        at = length - 1 - k if reverse else k
-        reached = at > position if reverse else at < position
-        new = combine(before, jax.tree.map(lambda part: part[at], everything))
-        return jax.tree.map(lambda a, b: jnp.where(reached, a, b), new, before)
-
-    return lax.fori_loop(0, length, hop, start)
 
 
 def lagrange(displace):
@@ -75,19 +57,47 @@
     return running_total
 
 
-def compose(earlier, latter):
-    product = jnp.einsum("...ij,...jk->...ik", latter, earlier, precision=PRECISE)
-    return product / product[..., 1:2, 1:2]
-
-
-def chain_affine(earlier, latter):
-    return (latter[0] * earlier[0], latter[0][..., None, :, None] * earlier[1] + latter[1])
-
-
-def mobius(lead_left, tail_left, lead_right, tail_right):
-    upper_row = jnp.stack([tail_left * lead_right - tail_right * lead_left, tail_right], axis=-1)
-    lower_row = jnp.stack([-lead_left, jnp.ones_like(lead_left)], axis=-1)
-    return jnp.stack([upper_row, lower_row], axis=-2)
+def interface_solve(packed_all, position, width):
+    count = packed_all.shape[0]
+    p = None
+    q = None
+    alphas, betas, lefts_p, lefts_q = [], [], [], []
+    for j in range(count):
+        first_j = packed_all[j, 0:width]
+        last_j = packed_all[j, width : 2 * width]
+        coef = packed_all[j, 2 * width]
+        lead_left = coef[:, 0:1]
+        tail_left = coef[:, 1:2]
+        lead_right = coef[:, 2:3]
+        tail_right = coef[:, 3:4]
+        if p is None:
+            pivot = jnp.ones_like(lead_left)
+            alpha = first_j
+            beta = -lead_right
+            p_new = last_j
+            q_new = -tail_right
+        else:
+            pivot = 1.0 + lead_left * q
+            alpha = (first_j - lead_left * p) / pivot
+            beta = -lead_right / pivot
+            p_new = last_j - tail_left * p - tail_left * q * alpha
+            q_new = -(tail_left * q * beta) - tail_right
+        alphas.append(alpha)
+        betas.append(beta)
+        lefts_p.append(p)
+        lefts_q.append(q)
+        p, q = p_new, q_new
+    firsts = [None] * count
+    ahead = None
+    for j in range(count - 1, -1, -1):
+        firsts[j] = alphas[j] if ahead is None else alphas[j] + betas[j] * ahead
+        ahead = firsts[j]
+    zero = jnp.zeros_like(firsts[0])
+    left_values = [zero] + [lefts_p[j] + lefts_q[j] * firsts[j] for j in range(1, count)]
+    right_values = firsts[1:] + [zero]
+    left_value = jnp.stack(left_values)[position]
+    right_value = jnp.stack(right_values)[position]
+    return left_value, right_value
 
 
 def local(fields, shift_x, shift_y, block_offset, group_inverse, lower_coupling, upper_coupling):
@@ -129,35 +139,20 @@
     upper_here = upper_coupling[:, 0]
     left_spike = group_inverse[:, :, 0] * lower_here[:, None]
     right_spike = group_inverse[:, :, columns - 1] * upper_here[:, None]
-    lead_left = left_spike[:, 0]
-    tail_left = left_spike[:, columns - 1]
-    lead_right = right_spike[:, 0]
-    tail_right = right_spike[:, columns - 1]
+    coef = jnp.stack(
+        [left_spike[:, 0], left_spike[:, columns - 1], right_spike[:, 0], right_spike[:, columns - 1]],
+        axis=-1,
+    )
+    coef_rows = jnp.pad(coef, ((0, 0), (0, rows_here - 4)))
     first_row = local_solve[:, :, 0, :]
     last_row = local_solve[:, :, columns - 1, :]
-    identity_map = jnp.broadcast_to(jnp.eye(2, dtype=jnp.float32), (level_count, 2, 2))
-    ones_level = jnp.ones((level_count,), jnp.float32)
-    zeros_rows = jnp.zeros_like(first_row)
-    before = carried_in(
-        mobius(lead_left, tail_left, lead_right, tail_right), "gx", compose, identity_map, False
-    )
-    gain_here = before[:, 0, 1] / before[:, 1, 1]
-    pivot_here = 1.0 - lead_left * gain_here
-    ratio_here = tail_left * gain_here / pivot_here
-    forward_map = (
-        -(ratio_here * lead_left + tail_left),
-        ratio_here[None, :, None] * first_row + last_row,
-    )
-    behind = carried_in(forward_map, "gx", chain_affine, (ones_level, zeros_rows), False)[1]
-    lead_value = first_row - lead_left[None, :, None] * behind
-    backward_map = (-lead_right / pivot_here, lead_value / pivot_here[None, :, None])
-    ahead_value = carried_in(backward_map, "gx", chain_affine, (ones_level, zeros_rows), True)[1]
-    first_value = backward_map[1] + backward_map[0][None, :, None] * ahead_value
-    left_value = behind - gain_here[None, :, None] * first_value
+    packed = jnp.concatenate([first_row, last_row, coef_rows[None]], axis=0)
+    packed_all = lax.all_gather(packed, "gx")
+    left_value, right_value = interface_solve(packed_all, position, first_row.shape[0])
     wind_fields = (
         local_solve
         - left_spike[None, :, :, None] * left_value[:, :, None, :]
-        - right_spike[None, :, :, None] * ahead_value[:, :, None, :]
+        - right_spike[None, :, :, None] * right_value[:, :, None, :]
     )
     return (wind_fields, advected[2:4])
 

time: 849 us -> 532 us (0.63)
  blocking collectives: 355 us -> 49.9 us
  waiting for transfers between devices: 244 us -> 332 us
  local copies, waits for them, and re-layouts: 112 us -> 38 us
  other arithmetic: 82.8 us -> 62.8 us
    all_gather x5 -> x1, blocking collectives: 355 us -> 49.9 us  [local(): packed_all = lax.all_gather(packed, 'gx')]
    ppermute x4, waiting for transfers between devices: 244 us -> 332 us  [shifted_2(): lax.ppermute(value, axis, [(source, source + steps) for source in range(l...]
    mul x66 -> x4, local copies, waits for them, and re-layouts: 60.2 us -> 0.03 us  [the longest x2 0.02 us: local(): left_spike[None, :, :, None] * left_value[:, :, None, :]]
    select_n x96 -> x0, other arithmetic: 28.9 us -> none  [hop(): return jax.tree.map(lambda a, b: jnp.where(reached, a, b), new, before)]
    unnamed x37 -> x31, local copies, waits for them, and re-layouts: 20.6 us -> 19.4 us
  transfers between devices with their start and end apart: 8 -> 8, of which waited for: 2 -> 3; matrix products, arithmetic and copies ran while one was open for 6% -> 5% of each run, Pallas kernels for 0% -> 0%
where the time goes in v1:
time: 532 us; the launch traced here: 529 us
  waiting for transfers between devices  332 us (62%)
  other arithmetic  62.8 us (12%)
  blocking collectives  49.9 us (9%)
  local copies, waits for them, and re-layouts  38 us (7%)
  starting transfers between devices  29.5 us (6%)
  between operations  15.7 us (3%)
    ppermute x4, waiting for transfers between devices, shifted_2(): lax.ppermute(value, axis, [(source, source + steps) for source in range(l...  332 us
    all_gather x1, blocking collectives, local(): packed_all = lax.all_gather(packed, 'gx')  49.9 us
    transpose x1, other arithmetic, local(): interpolated.transpose(1, 2, 0, 3, 4)  38.3 us
    unnamed x31, local copies, waits for them, and re-layouts  19.4 us
    ppermute x4, starting transfers between devices, shifted_2(): lax.ppermute(value, axis, [(source, source + steps) for source in range(l...  16 us
  transfers between devices with their start and end apart: 8, of which 3 were waited for; matrix products, arithmetic and copies ran while one was open for 5% of the time, Pallas kernels for 0%

profile of v1, /device:TPU:34, one launch (start us, length us, event | category | flops | bytes accessed | tf_op | source)
XLA Modules:
  0.0 529.2 jit_solution(17495697802358487689)
XLA Ops:
  0.6 1.0 fusion.239
  1.6 3.5 collective-permute-start
  5.1 4.5 collective-permute-start.1
  9.6 2.8 constant_dynamic-update-slice_fusion.1
  12.5 2.7 fusion.237
  15.1 2.8 copy.76
  18.0 1.9 collective-permute-start.2
  19.9 2.8 copy.77
  22.7 3.6 collective-permute-start.3
  26.4 2.6 copy.78
  29.0 2.6 copy.79
  31.5 6.1 %pad_maximum_fusion = f32[4,8,132,132]{3,1,2,0:T(8,128)} fusion(f32[4,8,132,2]{3,1,2,0:T(8,128)} %copy.79, f32[4,8,132,128]{3,1,2,0:T(8,128)S(1)} %constant_dynamic-update-slice_fusion, f32[4,8,132,2]{3,1,2,0:T(8,128)} %copy.78), kind=kLoop, calls=%fused_computation | loop fusion | flops 1115136 | bytes 4460544 | tf_op jit(solution)/shard_map/concatenate | solution.py:21
  37.6 3.4 collective-permute-start.4
  41.1 5.0 collective-permute-start.5
  46.1 0.7 fusion.244
  56.5 0.8 neg.203
  57.4 0.8 neg.206
  63.9 3.0 collective-permute-start.6
  67.0 4.6 collective-permute-start.7
  71.6 4.4 fusion.33
  76.0 63.5 %collective-permute-done.4 = f32[4,8,132,132]{3,1,2,0:T(8,128)} collective-permute-done((f32[4,8,132,132]{3,1,2,0:T(8,128)}, f32[4,8,132,132]{3,1,2,0:T(8,128)}, u32[]{:S(2)}, u32[]{:S(2)}) %collective-permute-start.4) | collective-permute-done | bytes 2230304 | tf_op jit(solution)/shard_map/ppermute | solution.py:28
  139.5 2.6 slice_dynamic-update-slice_fusion.1
  142.1 89.3 %collective-permute-done.5 = f32[4,8,132,132]{3,1,2,0:T(8,128)} collective-permute-done((f32[4,8,132,132]{3,1,2,0:T(8,128)}, f32[4,8,132,132]{3,1,2,0:T(8,128)}, u32[]{:S(2)}, u32[]{:S(2)}) %collective-permute-start.5) | collective-permute-done | bytes 2230304 | tf_op jit(solution)/shard_map/ppermute | solution.py:28
  231.4 2.8 slice_dynamic-update-slice_fusion.4
  234.2 2.8 slice_dynamic-update-slice_fusion.3
  237.1 179.4 %collective-permute-done.6 = f32[4,8,132,132]{3,1,2,0:T(8,128)S(1)} collective-permute-done((f32[4,8,132,132]{3,1,2,0:T(8,128)}, f32[4,8,132,132]{3,1,2,0:T(8,128)S(1)}, u32[]{:S(2)}, u32[]{:S(2)}) %collective-permute-start.6) | collective-permute-done | bytes 2230304 | tf_op jit(solution)/shard_map/ppermute | solution.py:28
  416.5 0.6 slice_dynamic-update-slice_fusion.2
  417.2 0.7 slice_dynamic-update-slice_fusion
  417.8 0.9 bitcast_dynamic-update-slice_fusion.7
  418.7 0.9 bitcast_dynamic-update-slice_fusion.6
  419.6 0.9 bitcast_dynamic-update-slice_fusion.5
  420.6 0.9 bitcast_dynamic-update-slice_fusion.4
  421.5 0.9 bitcast_dynamic-update-slice_fusion.3
  422.3 0.9 bitcast_dynamic-update-slice_fusion.2
  423.2 0.9 bitcast_dynamic-update-slice_fusion.1
  424.1 0.9 bitcast_dynamic-update-slice_fusion
  425.0 38.3 %fusion.3 = f32[4,8,8,16,128]{4,1,3,0,2:T(8,128)S(1)} fusion(f32[8,4,8,20,132]{4,2,3,1,0:T(8,128)} %bitcast_dynamic-update-slice_fusion, f32[8,8,16,128]{3,1,2,0:T(8,128)} %get-tuple-element.417, f32[8,8,16,128]{3,1,2,0:T(8,128)} %get-tuple-element.416, f32[8,8,16,128]{3,1,2,0:T(8,128)} %get-tuple-element.414, f32[8,8,16,128]{3,1,2,0:T(8,128)} %get-tuple-element.415, ...), kind=kLoop, calls=%fused_computation.10 | loop fusion | flops 28311552 | bytes 59768832 | tf_op jit(solution)/shard_map/transpose | solution.py:134
  463.7 1.1 convolution_bitcast_fusion
  464.9 49.9 %all-gather = f32[160,8,128]{2,1,0:T(8,128)S(1)} all-gather(f32[5,8,128]{2,1,0:T(8,128)S(1)} %copy.84), channel_id=2, replica_groups=mesh['gx'=32,'gy'=8] {'gx'}, dimensions={0}, use_global_device_ids=true | all-gather | bytes 675840 | tf_op jit(solution)/shard_map/all_gather | solution.py:150
  515.1 0.4 slice_subtract_fusion.61
  515.5 0.3 fusion.139
  515.8 0.3 fusion.202
  516.1 0.3 fusion.201
  516.3 0.3 fusion.200
  516.6 0.3 fusion.199
  516.9 0.3 fusion.198
  517.1 0.3 fusion.197
  517.4 0.3 fusion.196
  517.7 0.3 fusion.195
  517.9 0.3 fusion.194
  518.2 0.3 fusion.193
  519.2 0.3 fusion.189
  519.5 0.3 fusion.188
  519.8 0.3 fusion.187
  520.8 0.3 fusion.183
  521.1 0.3 fusion.182
  521.4 0.3 fusion.181
  521.6 0.3 fusion.180
  522.7 0.3 fusion.176
  522.9 0.3 fusion.175
  523.4 1.0 constant_dynamic-update-slice_fusion.33
  526.6 0.3 multiply_subtract_fusion
  527.0 1.0 copy.88
  528.0 1.2 copy.87
  (84 shorter events, 6.4 us)
Async XLA Ops:
  1.6 8.0 %collective-permute-start = (f32[4,8,2,128]{3,1,2,0:T(8,128)S(1)}, f32[4,8,2,128]{3,1,2,0:T(8,128)S(1)}, u32[]{:S(2)}, u32[]{:S(2)}) collective-permute-start(f32[4,8,2,128]{3,1,2,0:T(8,128)S(1)} %copy.104), channel_id=1, source_target_pairs={{0,8},{8,16},{16,24},{24,32},{32,40},{40,48},{48,56},{56,64},{64,7... | collective-permute-start | bytes 98312 | tf_op jit(solution)/shard_map/ppermute | solution.py:17
  5.1 7.3 %collective-permute-start.1 = (f32[4,8,2,128]{3,1,2,0:T(8,128)S(1)}, f32[4,8,2,128]{3,1,2,0:T(8,128)S(1)}, u32[]{:S(2)}, u32[]{:S(2)}) collective-permute-start(f32[4,8,2,128]{3,1,2,0:T(8,128)S(1)} %copy.105), channel_id=1, source_target_pairs={{8,0},{16,8},{24,16},{32,24},{40,32},{48,40},{56,48},{64,56},{72,6... | collective-permute-start | bytes 98312 | tf_op jit(solution)/shard_map/ppermute | solution.py:20
  18.0 8.4 %collective-permute-start.2 = (f32[4,8,132,2]{2,1,3,0:T(8,128)S(1)}, f32[4,8,132,2]{2,1,3,0:T(8,128)S(1)}, u32[]{:S(2)}, u32[]{:S(2)}) collective-permute-start(f32[4,8,132,2]{2,1,3,0:T(8,128)S(1)} %copy.76), channel_id=1, source_target_pairs={{0,1},{1,2},{2,3},{3,4},{4,5},{5,6},{6,7},{8,9},{9,10},{10,11},{11... | collective-permute-start | bytes 101384 | tf_op jit(solution)/shard_map/ppermute | solution.py:17
  22.7 6.2 %collective-permute-start.3 = (f32[4,8,132,2]{2,1,3,0:T(8,128)S(1)}, f32[4,8,132,2]{2,1,3,0:T(8,128)S(1)}, u32[]{:S(2)}, u32[]{:S(2)}) collective-permute-start(f32[4,8,132,2]{2,1,3,0:T(8,128)S(1)} %copy.77), channel_id=1, source_target_pairs={{1,0},{2,1},{3,2},{4,3},{5,4},{6,5},{7,6},{9,8},{10,9},{11,10},{12... | collective-permute-start | bytes 101384 | tf_op jit(solution)/shard_map/ppermute | solution.py:20
  31.5 9.5 %copy-start.5 = (s32[256,1]{0,1:T(1,128)S(1)}, s32[256,1]{0,1:T(1,128)}, u32[]{:S(2)}) copy-start(s32[256,1]{0,1:T(1,128)} %param.10) | copy-start | bytes 3076
  31.5 25.0 %copy-start.1 = (f32[8,128,128]{2,1,0:T(8,128)S(1)}, f32[8,128,128]{2,1,0:T(8,128)}, u32[]{:S(2)}) copy-start(f32[8,128,128]{2,1,0:T(8,128)} %param.8) | copy-start | bytes 1572868
  31.5 25.9 %copy-start.2 = (f32[8,128,128]{2,1,0:T(8,128)S(1)}, f32[8,128,128]{2,1,0:T(8,128)}, u32[]{:S(2)}) copy-start(f32[8,128,128]{2,1,0:T(8,128)} %param.9) | copy-start | bytes 1572868
  37.6 20.6 %copy-start = (f32[8,128,128]{2,1,0:T(8,128)S(1)}, f32[8,128,128]{2,1,0:T(8,128)}, u32[]{:S(2)}) copy-start(f32[8,128,128]{2,1,0:T(8,128)} %param.11) | copy-start | bytes 1572868
  37.6 101.9 %collective-permute-start.4 = (f32[4,8,132,132]{3,1,2,0:T(8,128)}, f32[4,8,132,132]{3,1,2,0:T(8,128)}, u32[]{:S(2)}, u32[]{:S(2)}) collective-permute-start(f32[4,8,132,132]{3,1,2,0:T(8,128)} %pad_maximum_fusion), channel_id=1, source_target_pairs={{0,16},{8,24},{16,32},{24,40},{32,48},{40,56},{48,64},{56,72},{64,... | collective-permute-start | bytes 6690824 | tf_op jit(solution)/shard_map/ppermute | solution.py:28
  41.1 190.3 %collective-permute-start.5 = (f32[4,8,132,132]{3,1,2,0:T(8,128)}, f32[4,8,132,132]{3,1,2,0:T(8,128)}, u32[]{:S(2)}, u32[]{:S(2)}) collective-permute-start(f32[4,8,132,132]{3,1,2,0:T(8,128)} %pad_maximum_fusion), channel_id=1, source_target_pairs={{0,8},{8,16},{16,24},{24,32},{32,40},{40,48},{48,56},{56,64},{64,7... | collective-permute-start | bytes 6690824 | tf_op jit(solution)/shard_map/ppermute | solution.py:28
  57.4 6.3 %copy-start.3 = (f32[8,1]{0,1:T(1,128)S(1)}, f32[8,1]{0,1:T(1,128)}, u32[]{:S(2)}) copy-start(f32[8,1]{0,1:T(1,128)} %param.13) | copy-start | bytes 100
  57.4 6.4 %copy-start.4 = (f32[8,1]{0,1:T(1,128)S(1)}, f32[8,1]{0,1:T(1,128)}, u32[]{:S(2)}) copy-start(f32[8,1]{0,1:T(1,128)} %param.12) | copy-start | bytes 100
  63.9 352.6 %collective-permute-start.6 = (f32[4,8,132,132]{3,1,2,0:T(8,128)}, f32[4,8,132,132]{3,1,2,0:T(8,128)S(1)}, u32[]{:S(2)}, u32[]{:S(2)}) collective-permute-start(f32[4,8,132,132]{3,1,2,0:T(8,128)} %pad_maximum_fusion), channel_id=1, source_target_pairs={{8,0},{16,8},{24,16},{32,24},{40,32},{48,40},{56,48},{64,56},{72,6... | collective-permute-start | bytes 6690824 | tf_op jit(solution)/shard_map/ppermute | solution.py:28
  67.0 350.2 %collective-permute-start.7 = (f32[4,8,132,132]{3,1,2,0:T(8,128)}, f32[4,8,132,132]{3,1,2,0:T(8,128)S(1)}, u32[]{:S(2)}, u32[]{:S(2)}) collective-permute-start(f32[4,8,132,132]{3,1,2,0:T(8,128)} %pad_maximum_fusion), channel_id=1, source_target_pairs={{16,0},{24,8},{32,16},{40,24},{48,32},{56,40},{64,48},{72,56},{80,... | collective-permute-start | bytes 6690824 | tf_op jit(solution)/shard_map/ppermute | solution.py:28

commit v2 on v1

--- a/solution.py
+++ b/solution.py
@@ -100,34 +100,94 @@
     return left_value, right_value
 
 
+def halo_x(block, axis, width):
+    count = lax.axis_size(axis)
+    forward = [(i, i + 1) for i in range(count - 1)]
+    backward = [(target, source) for source, target in forward]
+    low = lax.ppermute(block[:, block.shape[1] - width :], axis, forward)
+    high = lax.ppermute(block[:, 0:width], axis, backward)
+    return jnp.concatenate([low, block, high], axis=1)
+
+
+def halo_y(block, axis, width):
+    count = lax.axis_size(axis)
+    forward = [(i, i + 1) for i in range(count - 1)]
+    backward = [(target, source) for source, target in forward]
+    low = lax.ppermute(block[:, :, block.shape[2] - width :], axis, forward)
+    high = lax.ppermute(block[:, :, 0:width], axis, backward)
+    return jnp.concatenate([low, high], axis=2)
+
+
+def source_of(offsets, run, block_count):
+    blocks = run * block_count + jnp.arange(block_count, dtype=jnp.int32)
+    return blocks - lax.dynamic_slice_in_dim(offsets, run * block_count, block_count)
+
+
+def slot_rank(mask):
+    return jnp.cumsum(mask.astype(jnp.int32)) - 1
+
+
 def local(fields, shift_x, shift_y, block_offset, group_inverse, lower_coupling, upper_coupling):
     field_count, level_count, columns, rows_here = fields.shape
     block_count = columns // BX
+    window = BX + 4
+    cap = 4
+    channels = field_count * level_count
+    count = lax.axis_size("gx")
     position = lax.axis_index("gx")
-    padded = padded_2(fields, (("gx", 2), ("gy", 3)), 2)
+    flat = fields.reshape(channels, columns, rows_here)
+    main = halo_x(flat, "gx", 2)
+    halo = halo_y(main, "gy", 2).transpose(0, 2, 1)
     offsets = block_offset[:, 0]
-    inside = jnp.arange(block_count, dtype=jnp.int32)
-    own_offset = lax.dynamic_slice_in_dim(offsets, position * block_count, block_count)
-    shifted = []
-    for step_distance in (2, 1, -1, -2):
-        shifted.append(shifted_2(padded, "gx", step_distance))
-    window_field = jnp.concatenate(
-        [
-            shifted[0][:, :, 0 : columns + 2],
-            shifted[1][:, :, 2 : columns + 2],
-            padded[:, :, 2 : columns + 2],
-            shifted[2][:, :, 2 : columns + 2],
-            shifted[3][:, :, 2 : columns + 4],
-        ],
-        axis=2,
-    )
-    starts = (inside - own_offset) * BX + 2 * columns
-    windows = jnp.stack(
-        [
-            lax.dynamic_slice_in_dim(window_field, starts[column_block], BX + 4, 2)
-            for column_block in range(block_count)
+    deltas = (-2, -1, 1, 2)
+    received_main = {}
+    received_halo = {}
+    for delta in deltas:
+        target = jnp.clip(position - delta, 0, count - 1)
+        source = source_of(offsets, target, block_count)
+        local_start = (source - position * block_count) * BX
+        mask = (source >= position * block_count) & (source < (position + 1) * block_count)
+        rank = slot_rank(mask)
+        starts = [
+            jnp.sum(jnp.where(mask & (rank == slot), local_start, 0)) for slot in range(cap)
         ]
-    )
+        send_main = jnp.concatenate(
+            [lax.dynamic_slice_in_dim(main, start, window, 1) for start in starts], axis=1
+        )
+        send_halo = jnp.concatenate(
+            [lax.dynamic_slice_in_dim(halo, start, window, 2) for start in starts], axis=2
+        )
+        received_main[delta] = shifted_2(send_main, "gx", -delta)
+        received_halo[delta] = shifted_2(send_halo, "gx", -delta)
+    order = (-2, -1, 0, 1, 2)
+    pieces_main = [main if delta == 0 else received_main[delta] for delta in order]
+    pieces_halo = [halo if delta == 0 else received_halo[delta] for delta in order]
+    bases = {}
+    base = 0
+    for delta, piece in zip(order, pieces_main):
+        bases[delta] = base
+        base += piece.shape[1]
+    all_main = jnp.concatenate(pieces_main, axis=1)
+    all_halo = jnp.concatenate(pieces_halo, axis=2)
+    own_source = source_of(offsets, position, block_count)
+    own_delta = own_source // block_count - position
+    start_here = jnp.zeros((block_count,), jnp.int32)
+    for delta in order:
+        if delta == 0:
+            candidate = bases[0] + (own_source - position * block_count) * BX
+        else:
+            rank = slot_rank(own_delta == delta)
+            candidate = bases[delta] + rank * window
+        start_here = jnp.where(own_delta == delta, candidate, start_here)
+    window_main = jnp.stack(
+        [lax.dynamic_slice_in_dim(all_main, start_here[b], window, 1) for b in range(block_count)]
+    )
+    window_halo = jnp.stack(
+        [lax.dynamic_slice_in_dim(all_halo, start_here[b], window, 2) for b in range(block_count)]
+    ).transpose(0, 1, 3, 2)
+    windows = jnp.concatenate(
+        [window_halo[..., 0:2], window_main, window_halo[..., 2:4]], axis=3
+    ).reshape(block_count, field_count, level_count, window, rows_here + 4)
     across = shift_x.reshape(level_count, block_count, BX, rows_here).transpose(1, 0, 2, 3)[:, None]
     along = shift_y.reshape(level_count, block_count, BX, rows_here).transpose(1, 0, 2, 3)[:, None]
     interpolated = interpolate(windows, across, along, BX, rows_here)

time: 532 us -> 334 us (0.63)
  waiting for transfers between devices: 332 us -> 52.4 us
  blocking collectives: 49.9 us -> 80.6 us
  between operations: 15.7 us -> 46.2 us
  starting transfers between devices: 29.5 us -> 38.6 us
  other arithmetic: 62.8 us -> 69.1 us
    ppermute x4 -> x8, waiting for transfers between devices: 332 us -> 52.4 us  [shifted_2(): lax.ppermute(value, axis, [(source, source + steps) for source in range(l...]
    all_gather x1, blocking collectives: 49.9 us -> 80.6 us  [local(): packed_all = lax.all_gather(packed, 'gx')]
    concatenate x2 -> x7, local copies, waits for them, and re-layouts: 0.69 us -> 9.35 us  [the longest x4 7.47 us: local(): jnp.concatenate([lax.dynamic_slice_in_dim(main, start, window, 1) for sta...]
    ppermute x4 -> x8, starting transfers between devices: 16 us -> 24.6 us  [shifted_2(): lax.ppermute(value, axis, [(source, source + steps) for source in range(l...]
    unnamed x31 -> x59, local copies, waits for them, and re-layouts: 19.4 us -> 17.3 us
    slice x5 -> x8, local copies, waits for them, and re-layouts: 9.96 us -> 11.2 us  [the longest x2 3.8 us: halo_y(): high = lax.ppermute(block[:, :, 0:width], axis, backward)]
  transfers between devices with their start and end apart: 8 -> 12, of which waited for: 3 -> 3; matrix products, arithmetic and copies ran while one was open for 5% -> 13% of each run, Pallas kernels for 0% -> 0%
where the time goes in v2:
time: 334 us; the launch traced here: 331 us
  blocking collectives  80.6 us (24%)
  other arithmetic  69.1 us (21%)
  waiting for transfers between devices  52.4 us (16%)
  between operations  46.2 us (14%)
  local copies, waits for them, and re-layouts  43 us (13%)
  starting transfers between devices  38.6 us (12%)
    all_gather x1, blocking collectives, local(): packed_all = lax.all_gather(packed, 'gx')  80.6 us
    ppermute x8, waiting for transfers between devices, shifted_2(): lax.ppermute(value, axis, [(source, source + steps) for source in range(l...  52.4 us
    transpose x1, other arithmetic, local(): interpolated.transpose(1, 2, 0, 3, 4)  38.9 us
    ppermute x8, starting transfers between devices, shifted_2(): lax.ppermute(value, axis, [(source, source + steps) for source in range(l...  24.6 us
    unnamed x59, local copies, waits for them, and re-layouts  17.3 us
    div x29, other arithmetic, interface_solve(): beta = -lead_right / pivot  7.65 us
    concatenate x4, local copies, waits for them, and re-layouts, local(): jnp.concatenate([lax.dynamic_slice_in_dim(main, start, window, 1) for sta...  7.47 us
  transfers between devices with their start and end apart: 12, of which 3 were waited for; matrix products, arithmetic and copies ran while one was open for 13% of the time, Pallas kernels for 0%

profile of v2, /device:TPU:34, one launch (start us, length us, event | category | flops | bytes accessed | tf_op | source)
XLA Modules:
  0.0 331.0 jit_solution(2113692109459529212)
XLA Ops:
  0.6 2.8 copy.224
  3.5 3.6 %collective-permute-start = (f32[32,2,128]{2,0,1:T(8,128)S(1)}, f32[32,2,128]{2,0,1:T(8,128)S(1)}, u32[]{:S(2)}, u32[]{:S(2)}) collective-permute-start(f32[32,2,128]{2,0,1:T(8,128)S(1)} %get-tuple-element.329), channel_id=1, source_target_pairs={{0,8},{8,16},{16,24},{24,32},{32,40},{40,48},{48,56},{56,64},{64,7... | collective-permute-start | bytes 98312 | tf_op jit(solution)/shard_map/ppermute | solution.py:107
  7.1 4.5 %collective-permute-start.1 = (f32[32,2,128]{2,0,1:T(8,128)S(1)}, f32[32,2,128]{2,0,1:T(8,128)S(1)}, u32[]{:S(2)}, u32[]{:S(2)}) collective-permute-start(f32[32,2,128]{2,0,1:T(8,128)S(1)} %get-tuple-element.330), channel_id=1, source_target_pairs={{8,0},{16,8},{24,16},{32,24},{40,32},{48,40},{56,48},{64,56},{72,6... | collective-permute-start | bytes 98312 | tf_op jit(solution)/shard_map/ppermute | solution.py:108
  11.6 0.6 constant_dynamic-update-slice_fusion.44
  13.9 0.7 fusion.277
  14.6 1.1 neg.203
  15.7 1.9 neg.206
  17.6 1.1 fusion.273
  18.7 1.2 copy.206
  19.9 1.2 copy.204
  21.2 5.0 %fusion.33 = (f32[8,8,16,128]{3,1,2,0:T(8,128)}, f32[8,8,16,128]{3,1,2,0:T(8,128)}, f32[8,8,16,128]{3,1,2,0:T(8,128)}, f32[8,8,16,128]{3,1,2,0:T(8,128)}, f32[8,...) fusion(f32[8,8,16,128]{3,2,1,0:T(8,128)} %bitcast.435, ...), kind=kLoop, calls=%fused_computation.79 | loop fusion | flops 9175040 | bytes 6291456 | tf_op jit(solution)/shard_map/mul | solution.py:38
  26.3 0.8 fusion.190
  27.1 0.8 fusion.198
  73.0 2.1 fusion.269
  75.1 1.8 constant_dynamic-slice_fusion.5
  77.0 1.8 copy.187
  78.8 2.5 collective-permute-start.11
  81.4 3.2 copy.174
  84.6 1.9 collective-permute-start.2
  86.5 1.7 copy.175
  88.3 4.0 %collective-permute-start.3 = (f32[32,132,2]{1,0,2:T(8,128)S(1)}, f32[32,132,2]{1,0,2:T(8,128)S(1)}, u32[]{:S(2)}, u32[]{:S(2)}) collective-permute-start(f32[32,132,2]{1,0,2:T(8,128)S(1)} %copy.175), channel_id=1, source_target_pairs={{1,0},{2,1},{3,2},{4,3},{5,4},{6,5},{7,6},{9,8},{10,9},{11,10},{12... | collective-permute-start | bytes 101384 | tf_op jit(solution)/shard_map/ppermute | solution.py:117
  92.2 1.4 pad_maximum_fusion.3
  93.8 0.9 constant_dynamic-update-slice_fusion.1
  94.7 0.4 dynamic-slice_bitcast_fusion.3
  95.3 1.9 collective-permute-start.7
  97.3 3.0 collective-permute-start.6
  100.4 2.9 collective-permute-start.5
  103.4 5.4 %collective-permute-start.4 = (f32[32,4,80]{2,0,1:T(8,128)S(1)}, f32[32,4,80]{2,0,1:T(8,128)S(1)}, u32[]{:S(2)}, u32[]{:S(2)}) collective-permute-start(f32[32,4,80]{2,0,1:T(8,128)S(1)} %pad_maximum_fusion.5), channel_id=1, source_target_pairs={{0,16},{8,24},{16,32},{24,40},{32,48},{40,56},{48,64},{56,72},{64,... | collective-permute-start | bytes 122888 | tf_op jit(solution)/shard_map/ppermute | solution.py:28
  109.0 1.9 copy.186
  110.9 1.9 copy.185
  112.8 1.8 copy.184
  114.6 2.6 collective-permute-done.7
  117.3 1.9 collective-permute-start.10
  119.2 3.9 %collective-permute-start.9 = (f32[32,80,128]{2,1,0:T(8,128)}, f32[32,80,128]{2,1,0:T(8,128)}, u32[]{:S(2)}, u32[]{:S(2)}) collective-permute-start(f32[32,80,128]{2,1,0:T(8,128)} %copy.185), channel_id=1, source_target_pairs={{0,8},{8,16},{16,24},{24,32},{32,40},{40,48},{48,56},{56,64},{64,7... | collective-permute-start | bytes 3932168 | tf_op jit(solution)/shard_map/ppermute | solution.py:28
  123.1 3.1 collective-permute-start.8
  127.7 1.1 copy.192
  128.9 2.2 copy.193
  131.1 48.2 %collective-permute-done.8 = f32[32,80,128]{2,1,0:T(8,128)} collective-permute-done((f32[32,80,128]{2,1,0:T(8,128)}, f32[32,80,128]{2,1,0:T(8,128)}, u32[]{:S(2)}, u32[]{:S(2)}) %collective-permute-start.8) | collective-permute-done | bytes 1310752 | tf_op jit(solution)/shard_map/ppermute | solution.py:28
  179.3 1.7 copy_dynamic-update-slice_fusion.3
  181.1 1.5 collective-permute-done.9
  182.6 1.7 copy_dynamic-update-slice_fusion.2
  184.3 1.2 constant_dynamic-update-slice_fusion.11
  185.5 1.7 copy_dynamic-update-slice_fusion.1
  187.2 1.7 copy_dynamic-update-slice_fusion
  189.3 1.5 copy-done
  190.8 4.4 %maximum_bitcast_fusion = f32[8,4,8,20,132]{4,2,1,3,0:T(8,128)} fusion(f32[8,32,20,2]{3,1,2,0:T(8,128)S(1)} %copy-done, f32[8,32,20,128]{3,1,2,0:T(8,128)S(1)} %bitcast_dynamic-update-slice_fusion, f32[8,32,20,2]{3,1,2,0:T(8,128)S(1)} %copy.192), kind=kLoop, calls=%fused_computation | loop fusion | flops 1351680 | bytes 5406720 | tf_op jit(solution)/shard_map/reshape | solution.py:190
  195.2 38.9 %fusion.3 = f32[4,8,8,16,128]{4,1,0,3,2:T(8,128)S(1)} fusion(f32[8,4,8,20,132]{4,2,1,3,0:T(8,128)} %maximum_bitcast_fusion, f32[8,8,16,128]{3,1,2,0:T(8,128)} %get-tuple-element.507, f32[8,8,16,128]{3,1,2,0:T(8,128)} %get-tuple-element.506, f32[8,8,16,128]{3,1,2,0:T(8,128)} %get-tuple-element.504, f32[8,8,16,128]{3,1,2,0:T(8,128)} %get-tuple-element.505, ...), kind=kLoop, calls=%fused_computation.6 | loop fusion | flops 28311552 | bytes 59768832 | tf_op jit(solution)/shard_map/transpose | solution.py:194
  234.3 0.3 copy.194
  234.7 1.1 convolution_bitcast_fusion
  235.8 80.6 %all-gather = f32[160,8,128]{2,1,0:T(8,128)S(1)} all-gather(f32[5,8,128]{2,1,0:T(8,128)S(1)} %copy.198), channel_id=2, replica_groups=mesh['gx'=32,'gy'=8] {'gx'}, dimensions={0}, use_global_device_ids=true | all-gather | bytes 675840 | tf_op jit(solution)/shard_map/all_gather | solution.py:210
  316.7 0.4 slice_subtract_fusion.61
  317.2 0.3 fusion.157
  318.0 0.3 fusion.231
  318.2 0.3 fusion.230
  318.5 0.3 fusion.229
  318.7 0.3 fusion.228
  319.8 0.3 fusion.224
  320.1 0.3 fusion.223
  320.3 0.3 fusion.222
  321.4 0.3 fusion.218
  325.0 1.0 constant_dynamic-update-slice_fusion.43
  328.3 0.3 multiply_subtract_fusion
  328.6 1.0 copy.201
  329.7 1.3 copy.202
  (159 shorter events, 12.9 us)
Async XLA Ops:
  0.6 11.6 %copy-start.12 = (s32[256,1]{0,1:T(1,128)S(1)}, s32[256,1]{0,1:T(1,128)}, u32[]{:S(2)}) copy-start(s32[256,1]{0,1:T(1,128)} %param.10) | copy-start | bytes 3076
  3.5 14.1 %copy-start.2 = (f32[8,128,128]{2,1,0:T(8,128)S(1)}, f32[8,128,128]{2,1,0:T(8,128)}, u32[]{:S(2)}) copy-start(f32[8,128,128]{2,1,0:T(8,128)} %param.11) | copy-start | bytes 1572868
  3.5 69.3 %collective-permute-start = (f32[32,2,128]{2,0,1:T(8,128)S(1)}, f32[32,2,128]{2,0,1:T(8,128)S(1)}, u32[]{:S(2)}, u32[]{:S(2)}) collective-permute-start(f32[32,2,128]{2,0,1:T(8,128)S(1)} %get-tuple-element.329), channel_id=1, source_target_pairs={{0,8},{8,16},{16,24},{24,32},{32,40},{40,48},{48,56},{56,64},{64,7... | collective-permute-start | bytes 98312 | tf_op jit(solution)/shard_map/ppermute | solution.py:107
  7.1 65.7 %collective-permute-start.1 = (f32[32,2,128]{2,0,1:T(8,128)S(1)}, f32[32,2,128]{2,0,1:T(8,128)S(1)}, u32[]{:S(2)}, u32[]{:S(2)}) collective-permute-start(f32[32,2,128]{2,0,1:T(8,128)S(1)} %get-tuple-element.330), channel_id=1, source_target_pairs={{8,0},{16,8},{24,16},{32,24},{40,32},{48,40},{56,48},{64,56},{72,6... | collective-permute-start | bytes 98312 | tf_op jit(solution)/shard_map/ppermute | solution.py:108
  21.2 5.0 %copy-start.14 = (f32[8,1]{0,1:T(1,128)S(1)}, f32[8,1]{0,1:T(1,128)}, u32[]{:S(2)}) copy-start(f32[8,1]{0,1:T(1,128)} %param.13) | copy-start | bytes 100
  21.2 5.0 %copy-start.15 = (f32[8,1]{0,1:T(1,128)S(1)}, f32[8,1]{0,1:T(1,128)}, u32[]{:S(2)}) copy-start(f32[8,1]{0,1:T(1,128)} %param.12) | copy-start | bytes 100
  78.8 108.4 %collective-permute-start.11 = (f32[32,80,128]{2,1,0:T(8,128)}, f32[32,80,128]{2,1,0:T(8,128)}, u32[]{:S(2)}, u32[]{:S(2)}) collective-permute-start(f32[32,80,128]{2,1,0:T(8,128)} %copy.187), channel_id=1, source_target_pairs={{16,0},{24,8},{32,16},{40,24},{48,32},{56,40},{64,48},{72,56},{80,... | collective-permute-start | bytes 3932168 | tf_op jit(solution)/shard_map/ppermute | solution.py:28
  84.6 9.2 %collective-permute-start.2 = (f32[32,132,2]{1,0,2:T(8,128)S(1)}, f32[32,132,2]{1,0,2:T(8,128)}, u32[]{:S(2)}, u32[]{:S(2)}) collective-permute-start(f32[32,132,2]{1,0,2:T(8,128)S(1)} %copy.174), channel_id=1, source_target_pairs={{0,1},{1,2},{2,3},{3,4},{4,5},{5,6},{6,7},{8,9},{9,10},{10,11},{11... | collective-permute-start | bytes 101384 | tf_op jit(solution)/shard_map/ppermute | solution.py:116
  88.2 5.4 %copy-start.8 = (f32[32,20,128]{2,0,1:T(8,128)S(1)}, f32[32,20,128]{2,0,1:T(8,128)}, u32[]{:S(2)}) copy-start(f32[32,20,128]{2,0,1:T(8,128)} %get-tuple-element.317) | copy-start | bytes 983044
  88.2 5.4 %copy-start.9 = (f32[32,20,128]{2,0,1:T(8,128)S(1)}, f32[32,20,128]{2,0,1:T(8,128)}, u32[]{:S(2)}) copy-start(f32[32,20,128]{2,0,1:T(8,128)} %get-tuple-element.318) | copy-start | bytes 983044
  88.3 5.4 %copy-start.10 = (f32[32,20,128]{2,0,1:T(8,128)S(1)}, f32[32,20,128]{2,0,1:T(8,128)}, u32[]{:S(2)}) copy-start(f32[32,20,128]{2,0,1:T(8,128)} %get-tuple-element.319) | copy-start | bytes 983044
  88.3 5.4 %copy-start.11 = (f32[32,20,128]{2,0,1:T(8,128)S(1)}, f32[32,20,128]{2,0,1:T(8,128)}, u32[]{:S(2)}) copy-start(f32[32,20,128]{2,0,1:T(8,128)} %get-tuple-element.320) | copy-start | bytes 983044
  88.3 6.4 %collective-permute-start.3 = (f32[32,132,2]{1,0,2:T(8,128)S(1)}, f32[32,132,2]{1,0,2:T(8,128)S(1)}, u32[]{:S(2)}, u32[]{:S(2)}) collective-permute-start(f32[32,132,2]{1,0,2:T(8,128)S(1)} %copy.175), channel_id=1, source_target_pairs={{1,0},{2,1},{3,2},{4,3},{5,4},{6,5},{7,6},{9,8},{10,9},{11,10},{12... | collective-permute-start | bytes 101384 | tf_op jit(solution)/shard_map/ppermute | solution.py:117
  93.8 15.1 %copy-start.6 = (f32[32,20,128]{2,0,1:T(8,128)S(1)}, f32[32,20,128]{2,0,1:T(8,128)}, u32[]{:S(2)}) copy-start(f32[32,20,128]{2,0,1:T(8,128)} %get-tuple-element.323) | copy-start | bytes 983044
  93.8 15.1 %copy-start.7 = (f32[32,20,128]{2,0,1:T(8,128)S(1)}, f32[32,20,128]{2,0,1:T(8,128)}, u32[]{:S(2)}) copy-start(f32[32,20,128]{2,0,1:T(8,128)} %get-tuple-element.324) | copy-start | bytes 983044
  95.3 22.0 %collective-permute-start.7 = (f32[32,4,80]{2,0,1:T(8,128)S(1)}, f32[32,4,80]{2,0,1:T(8,128)S(1)}, u32[]{:S(2)}, u32[]{:S(2)}) collective-permute-start(f32[32,4,80]{2,0,1:T(8,128)S(1)} %pad_maximum_fusion.8), channel_id=1, source_target_pairs={{16,0},{24,8},{32,16},{40,24},{48,32},{56,40},{64,48},{72,56},{80,... | collective-permute-start | bytes 122888 | tf_op jit(solution)/shard_map/ppermute | solution.py:28
  97.3 21.9 %collective-permute-start.6 = (f32[32,4,80]{2,0,1:T(8,128)S(1)}, f32[32,4,80]{2,0,1:T(8,128)S(1)}, u32[]{:S(2)}, u32[]{:S(2)}) collective-permute-start(f32[32,4,80]{2,0,1:T(8,128)S(1)} %pad_maximum_fusion.7), channel_id=1, source_target_pairs={{8,0},{16,8},{24,16},{32,24},{40,32},{48,40},{56,48},{64,56},{72,6... | collective-permute-start | bytes 122888 | tf_op jit(solution)/shard_map/ppermute | solution.py:28
  100.4 22.7 %collective-permute-start.5 = (f32[32,4,80]{2,0,1:T(8,128)S(1)}, f32[32,4,80]{2,0,1:T(8,128)S(1)}, u32[]{:S(2)}, u32[]{:S(2)}) collective-permute-start(f32[32,4,80]{2,0,1:T(8,128)S(1)} %pad_maximum_fusion.6), channel_id=1, source_target_pairs={{0,8},{8,16},{16,24},{24,32},{32,40},{40,48},{48,56},{56,64},{64,7... | collective-permute-start | bytes 122888 | tf_op jit(solution)/shard_map/ppermute | solution.py:28
  103.4 22.8 %collective-permute-start.4 = (f32[32,4,80]{2,0,1:T(8,128)S(1)}, f32[32,4,80]{2,0,1:T(8,128)S(1)}, u32[]{:S(2)}, u32[]{:S(2)}) collective-permute-start(f32[32,4,80]{2,0,1:T(8,128)S(1)} %pad_maximum_fusion.5), channel_id=1, source_target_pairs={{0,16},{8,24},{16,32},{24,40},{32,48},{40,56},{48,64},{56,72},{64,... | collective-permute-start | bytes 122888 | tf_op jit(solution)/shard_map/ppermute | solution.py:28
  117.3 68.3 %collective-permute-start.10 = (f32[32,80,128]{2,1,0:T(8,128)}, f32[32,80,128]{2,1,0:T(8,128)}, u32[]{:S(2)}, u32[]{:S(2)}) collective-permute-start(f32[32,80,128]{2,1,0:T(8,128)} %copy.186), channel_id=1, source_target_pairs={{8,0},{16,8},{24,16},{32,24},{40,32},{48,40},{56,48},{64,56},{72,6... | collective-permute-start | bytes 3932168 | tf_op jit(solution)/shard_map/ppermute | solution.py:28
  119.2 63.4 %collective-permute-start.9 = (f32[32,80,128]{2,1,0:T(8,128)}, f32[32,80,128]{2,1,0:T(8,128)}, u32[]{:S(2)}, u32[]{:S(2)}) collective-permute-start(f32[32,80,128]{2,1,0:T(8,128)} %copy.185), channel_id=1, source_target_pairs={{0,8},{8,16},{16,24},{24,32},{32,40},{40,48},{48,56},{56,64},{64,7... | collective-permute-start | bytes 3932168 | tf_op jit(solution)/shard_map/ppermute | solution.py:28
  123.1 56.2 %collective-permute-start.8 = (f32[32,80,128]{2,1,0:T(8,128)}, f32[32,80,128]{2,1,0:T(8,128)}, u32[]{:S(2)}, u32[]{:S(2)}) collective-permute-start(f32[32,80,128]{2,1,0:T(8,128)} %copy.184), channel_id=1, source_target_pairs={{0,16},{8,24},{16,32},{24,40},{32,48},{40,56},{48,64},{56,72},{64,... | collective-permute-start | bytes 3932168 | tf_op jit(solution)/shard_map/ppermute | solution.py:28
  131.1 53.2 %copy-start.1 = (f32[4,8,128,128]{3,2,1,0:T(8,128)S(1)}, f32[4,8,128,128]{3,2,1,0:T(8,128)}, u32[]{:S(2)}) copy-start(f32[4,8,128,128]{3,2,1,0:T(8,128)} %param.7) | copy-start | bytes 6291460
  189.0 1.7 copy-start
  190.8 4.4 %copy-start.3 = (f32[8,8,16,128]{3,1,2,0:T(8,128)S(1)}, f32[8,8,16,128]{3,1,2,0:T(8,128)}, u32[]{:S(2)}) copy-start(f32[8,8,16,128]{3,1,2,0:T(8,128)} %get-tuple-element.374) | copy-start | bytes 1572868
  190.8 4.4 %copy-start.4 = (f32[8,8,16,128]{3,1,2,0:T(8,128)S(1)}, f32[8,8,16,128]{3,1,2,0:T(8,128)}, u32[]{:S(2)}) copy-start(f32[8,8,16,128]{3,1,2,0:T(8,128)} %get-tuple-element.375) | copy-start | bytes 1572868
  190.8 4.4 %copy-start.5 = (f32[8,8,16,128]{3,1,2,0:T(8,128)S(1)}, f32[8,8,16,128]{3,1,2,0:T(8,128)}, u32[]{:S(2)}) copy-start(f32[8,8,16,128]{3,1,2,0:T(8,128)} %get-tuple-element.376) | copy-start | bytes 1572868
  234.7 90.3 %copy-start.13 = (f32[32,2,8,128]{3,2,1,0:T(8,128)S(1)}, f32[32,2,8,128]{3,2,1,0:T(8,128)}, u32[]{:S(2)}) copy-start(f32[32,2,8,128]{3,2,1,0:T(8,128)} %constant_dynamic-update-slice_fusion.44) | copy-start | bytes 786436

commit v3 on v2

--- a/solution.py
+++ b/solution.py
@@ -127,18 +127,10 @@
     return jnp.cumsum(mask.astype(jnp.int32)) - 1
 
 
-def local(fields, shift_x, shift_y, block_offset, group_inverse, lower_coupling, upper_coupling):
-    field_count, level_count, columns, rows_here = fields.shape
-    block_count = columns // BX
+def send_windows(main, halo, offsets, position, count, block_count):
     window = BX + 4
     cap = 4
-    channels = field_count * level_count
-    count = lax.axis_size("gx")
-    position = lax.axis_index("gx")
-    flat = fields.reshape(channels, columns, rows_here)
-    main = halo_x(flat, "gx", 2)
-    halo = halo_y(main, "gy", 2).transpose(0, 2, 1)
-    offsets = block_offset[:, 0]
+    channels, _, rows_here = main.shape
     deltas = (-2, -1, 1, 2)
     received_main = {}
     received_halo = {}
@@ -157,8 +149,16 @@
         send_halo = jnp.concatenate(
             [lax.dynamic_slice_in_dim(halo, start, window, 2) for start in starts], axis=2
         )
-        received_main[delta] = shifted_2(send_main, "gx", -delta)
-        received_halo[delta] = shifted_2(send_halo, "gx", -delta)
+        span = cap * window
+        send_halo = jnp.pad(send_halo, ((0, 0), (0, 0), (0, rows_here - span)))
+        sent = shifted_2(jnp.concatenate([send_main, send_halo], axis=1), "gx", -delta)
+        received_main[delta] = sent[:, 0:span]
+        received_halo[delta] = sent[:, span:, 0:span]
+    return received_main, received_halo
+
+
+def assemble_windows(main, halo, received_main, received_halo, offsets, position, block_count):
+    window = BX + 4
     order = (-2, -1, 0, 1, 2)
     pieces_main = [main if delta == 0 else received_main[delta] for delta in order]
     pieces_halo = [halo if delta == 0 else received_halo[delta] for delta in order]
@@ -185,16 +185,43 @@
     window_halo = jnp.stack(
         [lax.dynamic_slice_in_dim(all_halo, start_here[b], window, 2) for b in range(block_count)]
     ).transpose(0, 1, 3, 2)
-    windows = jnp.concatenate(
+    return jnp.concatenate(
         [window_halo[..., 0:2], window_main, window_halo[..., 2:4]], axis=3
-    ).reshape(block_count, field_count, level_count, window, rows_here + 4)
+    )
+
+
+def advect_group(windows, shift_x, shift_y, field_count):
+    block_count = windows.shape[0]
+    level_count, columns, rows_here = shift_x.shape
+    windows = windows.reshape(block_count, field_count, level_count, BX + 4, rows_here + 4)
     across = shift_x.reshape(level_count, block_count, BX, rows_here).transpose(1, 0, 2, 3)[:, None]
     along = shift_y.reshape(level_count, block_count, BX, rows_here).transpose(1, 0, 2, 3)[:, None]
     interpolated = interpolate(windows, across, along, BX, rows_here)
-    advected = interpolated.transpose(1, 2, 0, 3, 4).reshape(
+    return interpolated.transpose(1, 2, 0, 3, 4).reshape(
         field_count, level_count, columns, rows_here
     )
-    local_solve = jnp.einsum("lij,wljy->wliy", group_inverse, advected[0:2], precision=PRECISE)
+
+
+def local(fields, shift_x, shift_y, block_offset, group_inverse, lower_coupling, upper_coupling):
+    field_count, level_count, columns, rows_here = fields.shape
+    block_count = columns // BX
+    channels = field_count * level_count
+    wind_channels = 2 * level_count
+    count = lax.axis_size("gx")
+    position = lax.axis_index("gx")
+    flat = fields.reshape(channels, columns, rows_here)
+    main = halo_x(flat, "gx", 2)
+    halo = halo_y(main, "gy", 2).transpose(0, 2, 1)
+    offsets = block_offset[:, 0]
+    wind_main, wind_halo = main[:wind_channels], halo[:wind_channels]
+    tracer_main, tracer_halo = main[wind_channels:], halo[wind_channels:]
+    wind_received = send_windows(wind_main, wind_halo, offsets, position, count, block_count)
+    tracer_received = send_windows(tracer_main, tracer_halo, offsets, position, count, block_count)
+    wind_windows = assemble_windows(
+        wind_main, wind_halo, *wind_received, offsets, position, block_count
+    )
+    winds = advect_group(wind_windows, shift_x, shift_y, 2)
+    local_solve = jnp.einsum("lij,wljy->wliy", group_inverse, winds, precision=PRECISE)
     lower_here = lower_coupling[:, 0]
     upper_here = upper_coupling[:, 0]
     left_spike = group_inverse[:, :, 0] * lower_here[:, None]
@@ -208,13 +235,18 @@
     last_row = local_solve[:, :, columns - 1, :]
     packed = jnp.concatenate([first_row, last_row, coef_rows[None]], axis=0)
     packed_all = lax.all_gather(packed, "gx")
+    packed_all, tracer_received = lax.optimization_barrier((packed_all, tracer_received))
     left_value, right_value = interface_solve(packed_all, position, first_row.shape[0])
     wind_fields = (
         local_solve
         - left_spike[None, :, :, None] * left_value[:, :, None, :]
         - right_spike[None, :, :, None] * right_value[:, :, None, :]
     )
-    return (wind_fields, advected[2:4])
+    tracer_windows = assemble_windows(
+        tracer_main, tracer_halo, *tracer_received, offsets, position, block_count
+    )
+    tracers = advect_group(tracer_windows, shift_x, shift_y, field_count - 2)
+    return (wind_fields, tracers)
 
 
 def solution(mesh):

time: 334 us -> 289 us (0.87)
  blocking collectives: 80.6 us -> 52 us
  other arithmetic: 69.1 us -> 46.9 us
  waiting for transfers between devices: 52.4 us -> 36.9 us
  starting transfers between devices: 38.6 us -> 50.5 us
  local copies, waits for them, and re-layouts: 43 us -> 50.4 us
    transpose x1, other arithmetic: 38.9 us -> 0.01 us  [local(): halo = halo_y(main, 'gy', 2).transpose(0, 2, 1)]
    all_gather x1, blocking collectives: 80.6 us -> 52 us  [local(): packed_all = lax.all_gather(packed, 'gx')]
    ppermute x8, waiting for transfers between devices: 52.4 us -> 35.3 us  [shifted_2(): lax.ppermute(value, axis, [(source, source + steps) for source in range(l...]
    add x0 -> x2, other arithmetic: none -> 16 us  [interpolate(): running_total + tap_term]
    slice x6 -> x22, local copies, waits for them, and re-layouts: 4.69 us -> 17.1 us  [the longest x4 4.91 us: send_windows(): received_main[delta] = sent[:, 0:span]]
    ppermute x8, starting transfers between devices: 24.6 us -> 37 us  [shifted_2(): lax.ppermute(value, axis, [(source, source + steps) for source in range(l...]
    concatenate x7 -> x4, local copies, waits for them, and re-layouts: 9.35 us -> 0.34 us  [the longest x2 0.25 us: assemble_windows(): all_halo = jnp.concatenate(pieces_halo, axis=2)]
    unnamed x59 -> x85, local copies, waits for them, and re-layouts: 17.3 us -> 21.6 us
  transfers between devices with their start and end apart: 12 -> 12, of which waited for: 3 -> 4; matrix products, arithmetic and copies ran while one was open for 13% -> 18% of each run, Pallas kernels for 0% -> 0%
where the time goes in v3:
time: 289 us; the launch traced here: 286 us
  blocking collectives  52 us (18%)
  starting transfers between devices  50.5 us (17%)
  local copies, waits for them, and re-layouts  50.4 us (17%)
  other arithmetic  46.9 us (16%)
  between operations  46.7 us (16%)
  waiting for transfers between devices  36.9 us (13%)
    all_gather x1, blocking collectives, local(): packed_all = lax.all_gather(packed, 'gx')  52 us
    ppermute x8, starting transfers between devices, shifted_2(): lax.ppermute(value, axis, [(source, source + steps) for source in range(l...  37 us
    ppermute x8, waiting for transfers between devices, shifted_2(): lax.ppermute(value, axis, [(source, source + steps) for source in range(l...  35.3 us
    unnamed x85, local copies, waits for them, and re-layouts  21.6 us
    add x2, other arithmetic, interpolate(): running_total + tap_term  16 us
    div x29, other arithmetic, interface_solve(): beta = -lead_right / pivot  7.65 us
    reshape x2, other arithmetic, advect_group(): windows.reshape(block_count, field_count, level_count, BX + 4, rows_here...  6.42 us
    slice x2, local copies, waits for them, and re-layouts, halo_y(): low = lax.ppermute(block[:, :, block.shape[2] - width:], axis, forward)  6.1 us
  transfers between devices with their start and end apart: 12, of which 4 were waited for; matrix products, arithmetic and copies ran while one was open for 18% of the time, Pallas kernels for 0%

profile of v3, /device:TPU:34, one launch (start us, length us, event | category | flops | bytes accessed | tf_op | source)
XLA Modules:
  0.0 286.2 jit_solution(7728532205921911953)
XLA Ops:
  0.7 2.9 %copy.112 = f32[4,8,128,128]{3,1,0,2:T(8,128)S(1)} copy(f32[4,8,128,128]{3,2,1,0:T(8,128)} %param.7) | data formatting | bytes 4194304 | tf_op args[0]
  3.6 1.4 copy-done.2
  4.9 3.5 %collective-permute-start = (f32[32,2,128]{2,0,1:T(8,128)S(1)}, f32[32,2,128]{2,0,1:T(8,128)S(1)}, u32[]{:S(2)}, u32[]{:S(2)}) collective-permute-start(f32[32,2,128]{2,0,1:T(8,128)S(1)} %get-tuple-element.325), channel_id=1, source_target_pairs={{0,8},{8,16},{16,24},{24,32},{32,40},{40,48},{48,56},{56,64},{64,7... | collective-permute-start | bytes 98312 | tf_op jit(solution)/shard_map/ppermute | solution.py:107
  8.4 4.5 %collective-permute-start.1 = (f32[32,2,128]{2,0,1:T(8,128)S(1)}, f32[32,2,128]{2,0,1:T(8,128)S(1)}, u32[]{:S(2)}, u32[]{:S(2)}) collective-permute-start(f32[32,2,128]{2,0,1:T(8,128)S(1)} %get-tuple-element.326), channel_id=1, source_target_pairs={{8,0},{16,8},{24,16},{32,24},{40,32},{48,40},{56,48},{64,56},{72,6... | collective-permute-start | bytes 98312 | tf_op jit(solution)/shard_map/ppermute | solution.py:108
  15.3 3.9 %fusion.62 = (f32[8,8,16,128]{3,1,2,0:T(8,128)}, f32[8,8,16,128]{3,1,2,0:T(8,128)}, f32[8,8,16,128]{3,1,2,0:T(8,128)}, f32[8,8,16,128]{3,1,2,0:T(8,128)}, f32[8,...) fusion(f32[8,8,16,128]{3,2,1,0:T(8,128)S(1)} %bitcast.437, ...), kind=kLoop, calls=%fused_computation.130 | loop fusion | flops 9175040 | bytes 6291456 | tf_op jit(solution)/shard_map/mul | solution.py:38
  19.5 0.8 fusion.161
  20.3 0.8 fusion.169
  21.1 0.7 fusion.216
  67.1 1.8 pad_maximum_fusion
  68.9 2.9 %fusion.207 = (f32[32,132,2]{2,0,1:T(8,128)}, f32[32,132,2]{2,0,1:T(8,128)}) fusion(f32[32,132,128]{2,0,1:T(8,128)S(1)} %pad_maximum_fusion), kind=kLoop, calls=%fused_computation.858 | loop fusion | bytes 135168 | tf_op jit(solution)/shard_map/slice | solution.py:116
  71.9 3.2 %copy.80 = f32[32,132,2]{1,0,2:T(8,128)S(1)} copy(f32[32,132,2]{2,0,1:T(8,128)} %get-tuple-element.323) | data formatting | bytes 67584 | tf_op jit(solution)/shard_map/slice | solution.py:116
  75.1 1.9 collective-permute-start.2
  77.0 3.2 %copy.81 = f32[32,132,2]{1,0,2:T(8,128)S(1)} copy(f32[32,132,2]{2,0,1:T(8,128)} %get-tuple-element.324) | data formatting | bytes 67584 | tf_op jit(solution)/shard_map/slice | solution.py:117
  80.2 3.6 %collective-permute-start.3 = (f32[32,132,2]{1,0,2:T(8,128)S(1)}, f32[32,132,2]{1,0,2:T(8,128)S(1)}, u32[]{:S(2)}, u32[]{:S(2)}) collective-permute-start(f32[32,132,2]{1,0,2:T(8,128)S(1)} %copy.81), channel_id=1, source_target_pairs={{1,0},{2,1},{3,2},{4,3},{5,4},{6,5},{7,6},{9,8},{10,9},{11,10},{12... | collective-permute-start | bytes 101384 | tf_op jit(solution)/shard_map/ppermute | solution.py:117
  84.1 1.6 collective-permute-done.3
  86.2 3.0 %collective-permute-start.4 = (f32[16,84,128]{2,0,1:T(8,128)S(1)}, f32[16,84,128]{2,0,1:T(8,128)S(1)}, u32[]{:S(2)}, u32[]{:S(2)}) collective-permute-start(f32[16,84,128]{2,0,1:T(8,128)S(1)} %constant_dynamic-update-slice_fusion), channel_id=1, source_target_pairs={{0,16},{8,24},{16,32},{24,40},{32,48},{40,56},{48,64},{56,72},{64,... | collective-permute-start | bytes 2064392 | tf_op jit(solution)/shard_map/ppermute | solution.py:28
  89.2 0.6 constant_dynamic-update-slice_fusion.88
  89.9 2.6 collective-permute-start.5
  92.7 5.4 %collective-permute-start.6 = (f32[16,84,128]{2,0,1:T(8,128)S(1)}, f32[16,84,128]{2,0,1:T(8,128)S(1)}, u32[]{:S(2)}, u32[]{:S(2)}) collective-permute-start(f32[16,84,128]{2,0,1:T(8,128)S(1)} %constant_dynamic-update-slice_fusion.10), channel_id=1, source_target_pairs={{8,0},{16,8},{24,16},{32,24},{40,32},{48,40},{56,48},{64,56},{72,6... | collective-permute-start | bytes 2064392 | tf_op jit(solution)/shard_map/ppermute | solution.py:28
  98.1 3.3 %collective-permute-start.7 = (f32[16,84,128]{2,0,1:T(8,128)S(1)}, f32[16,84,128]{2,0,1:T(8,128)S(1)}, u32[]{:S(2)}, u32[]{:S(2)}) collective-permute-start(f32[16,84,128]{2,0,1:T(8,128)S(1)} %constant_dynamic-update-slice_fusion.15), channel_id=1, source_target_pairs={{16,0},{24,8},{32,16},{40,24},{48,32},{56,40},{64,48},{72,56},{80,... | collective-permute-start | bytes 2064392 | tf_op jit(solution)/shard_map/ppermute | solution.py:28
  101.8 7.3 %collective-permute-done.4 = f32[16,84,128]{2,0,1:T(8,128)S(1)} collective-permute-done((f32[16,84,128]{2,0,1:T(8,128)S(1)}, f32[16,84,128]{2,0,1:T(8,128)S(1)}, u32[]{:S(2)}, u32[]{:S(2)}) %collective-permute-start.4) | collective-permute-done | bytes 688160 | tf_op jit(solution)/shard_map/ppermute | solution.py:28
  109.1 13.9 %collective-permute-done.5 = f32[16,84,128]{2,0,1:T(8,128)S(1)} collective-permute-done((f32[16,84,128]{2,0,1:T(8,128)S(1)}, f32[16,84,128]{2,0,1:T(8,128)S(1)}, u32[]{:S(2)}, u32[]{:S(2)}) %collective-permute-start.5) | collective-permute-done | bytes 688160 | tf_op jit(solution)/shard_map/ppermute | solution.py:28
  123.2 0.9 constant_dynamic-update-slice_fusion.56
  124.0 0.9 constant_dynamic-update-slice_fusion.55
  124.9 0.9 constant_dynamic-update-slice_fusion.54
  125.8 0.9 constant_dynamic-update-slice_fusion.53
  126.6 0.7 constant_dynamic-update-slice_fusion.52
  127.3 2.2 collective-permute-start.11
  129.5 0.7 constant_dynamic-update-slice_fusion.47
  130.2 15.9 %collective-permute-start.10 = (f32[16,84,128]{2,0,1:T(8,128)}, f32[16,84,128]{2,0,1:T(8,128)}, u32[]{:S(2)}, u32[]{:S(2)}) collective-permute-start(f32[16,84,128]{2,0,1:T(8,128)} %constant_dynamic-update-slice_fusion.47), channel_id=1, source_target_pairs={{8,0},{16,8},{24,16},{32,24},{40,32},{48,40},{56,48},{64,56},{72,6... | collective-permute-start | bytes 2064392 | tf_op jit(solution)/shard_map/ppermute | solution.py:28
  146.1 0.7 constant_dynamic-update-slice_fusion.42
  146.8 2.8 collective-permute-start.9
  149.6 0.7 constant_dynamic-update-slice_fusion.37
  150.3 14.1 %collective-permute-done.6 = f32[16,84,128]{2,0,1:T(8,128)S(1)} collective-permute-done((f32[16,84,128]{2,0,1:T(8,128)S(1)}, f32[16,84,128]{2,0,1:T(8,128)S(1)}, u32[]{:S(2)}, u32[]{:S(2)}) %collective-permute-start.6) | collective-permute-done | bytes 688160 | tf_op jit(solution)/shard_map/ppermute | solution.py:28
  164.4 1.9 collective-permute-start.8
  166.5 1.7 copy-done.11
  168.4 0.9 constant_dynamic-update-slice_fusion.35
  169.4 0.9 constant_dynamic-update-slice_fusion.34
  170.4 0.9 constant_dynamic-update-slice_fusion.33
  171.5 0.9 constant_dynamic-update-slice_fusion.32
  172.5 0.9 constant_dynamic-update-slice_fusion.31
  173.5 0.9 constant_dynamic-update-slice_fusion.30
  174.5 0.9 constant_dynamic-update-slice_fusion.29
  175.6 2.0 copy.82
  177.6 2.0 copy.83
  179.6 3.2 %maximum_bitcast_fusion = f32[8,2,8,20,132]{4,2,1,3,0:T(8,128)S(1)} fusion(f32[8,16,20,2]{3,1,2,0:T(8,128)} %copy.83, f32[8,16,20,128]{3,1,2,0:T(8,128)} %copy-done.9, f32[8,16,20,2]{3,1,2,0:T(8,128)} %copy.82), kind=kLoop, calls=%fused_computation | loop fusion | flops 675840 | bytes 2703360 | tf_op jit(solution)/shard_map/reshape | solution.py:196
  182.8 8.0 %fusion.31 = f32[8,2,8,16,128]{4,2,1,3,0:T(8,128)} fusion(f32[8,2,8,20,132]{4,2,1,3,0:T(8,128)S(1)} %maximum_bitcast_fusion, f32[8,8,16,128]{3,1,2,0:T(8,128)} %get-tuple-element.547, f32[8,8,16,128]{3,1,2,0:T(8,128)} %get-tuple-element.546, f32[8,8,16,128]{3,1,2,0:T(8,128)} %get-tuple-element.544, f32[8,8,16,128]{3,1,2,0:T(8,128)} %get-tuple-element.545, ...), kind=kLoop, calls=%fused_computation.62 | loop fusion | flops 14155776 | bytes 32505856 | tf_op jit(solution)/shard_map/add | solution.py:56
  190.8 2.7 convolution_bitcast_fusion
  193.6 52.0 %all-gather = f32[160,8,128]{2,1,0:T(8,128)S(1)} all-gather(f32[5,8,128]{2,1,0:T(8,128)S(1)} %copy.88), channel_id=2, replica_groups=mesh['gx'=32,'gy'=8] {'gx'}, dimensions={0}, use_global_device_ids=true | all-gather | bytes 675840 | tf_op jit(solution)/shard_map/all_gather | solution.py:237
  245.6 1.4 slice.1312
  247.0 0.8 slice.1316
  247.7 1.1 slice.1311
  248.9 0.8 slice.1315
  249.6 1.1 slice.1310
  250.8 0.8 slice.1314
  251.5 1.3 slice.1309
  252.8 0.8 slice.1313
  255.0 2.1 copy.91
  257.1 2.0 copy.92
  259.1 3.2 %maximum_bitcast_fusion.1 = f32[8,2,8,20,132]{4,2,1,3,0:T(8,128)S(1)} fusion(f32[8,16,20,2]{3,1,2,0:T(8,128)} %copy.92, f32[8,16,20,128]{3,1,2,0:T(8,128)} %copy-done.10, f32[8,16,20,2]{3,1,2,0:T(8,128)} %copy.91), kind=kLoop, calls=%fused_computation.1 | loop fusion | flops 675840 | bytes 2703360 | tf_op jit(solution)/shard_map/reshape | solution.py:196
  262.3 8.0 %fusion.2 = f32[8,2,8,16,128]{4,2,1,3,0:T(8,128)} fusion(f32[8,2,8,20,132]{4,2,1,3,0:T(8,128)S(1)} %maximum_bitcast_fusion.1, f32[8,8,16,128]{3,1,2,0:T(8,128)} %get-tuple-element.547, f32[8,8,16,128]{3,1,2,0:T(8,128)} %get-tuple-element.546, f32[8,8,16,128]{3,1,2,0:T(8,128)} %get-tuple-element.544, f32[8,8,16,128]{3,1,2,0:T(8,128)} %get-tuple-element.545, ...), kind=kLoop, calls=%fused_computation.8 | loop fusion | flops 14155776 | bytes 32505856 | tf_op jit(solution)/shard_map/add | solution.py:56
  270.3 2.6 copy.94
  281.5 1.0 constant_dynamic-update-slice_fusion.87
  285.1 1.0 copy.93
  (194 shorter events, 17.6 us)
Async XLA Ops:
  0.6 12.3 %copy-start.14 = (s32[256,1]{0,1:T(1,128)S(1)}, s32[256,1]{0,1:T(1,128)}, u32[]{:S(2)}) copy-start(s32[256,1]{0,1:T(1,128)} %param.10) | copy-start | bytes 3076
  0.6 13.9 %copy-start.12 = (f32[8,128,128]{2,1,0:T(8,128)S(1)}, f32[8,128,128]{2,1,0:T(8,128)}, u32[]{:S(2)}) copy-start(f32[8,128,128]{2,1,0:T(8,128)} %param.8) | copy-start | bytes 1572868
  0.7 14.0 %copy-start.13 = (f32[8,128,128]{2,1,0:T(8,128)S(1)}, f32[8,128,128]{2,1,0:T(8,128)}, u32[]{:S(2)}) copy-start(f32[8,128,128]{2,1,0:T(8,128)} %param.9) | copy-start | bytes 1572868
  3.6 1.4 copy-start.2
  3.6 11.1 %copy-start.4 = (f32[8,128,128]{2,1,0:T(8,128)S(1)}, f32[8,128,128]{2,1,0:T(8,128)}, u32[]{:S(2)}) copy-start(f32[8,128,128]{2,1,0:T(8,128)} %param.11) | copy-start | bytes 1572868
  4.9 62.1 %collective-permute-start = (f32[32,2,128]{2,0,1:T(8,128)S(1)}, f32[32,2,128]{2,0,1:T(8,128)S(1)}, u32[]{:S(2)}, u32[]{:S(2)}) collective-permute-start(f32[32,2,128]{2,0,1:T(8,128)S(1)} %get-tuple-element.325), channel_id=1, source_target_pairs={{0,8},{8,16},{16,24},{24,32},{32,40},{40,48},{48,56},{56,64},{64,7... | collective-permute-start | bytes 98312 | tf_op jit(solution)/shard_map/ppermute | solution.py:107
  8.4 58.6 %collective-permute-start.1 = (f32[32,2,128]{2,0,1:T(8,128)S(1)}, f32[32,2,128]{2,0,1:T(8,128)S(1)}, u32[]{:S(2)}, u32[]{:S(2)}) collective-permute-start(f32[32,2,128]{2,0,1:T(8,128)S(1)} %get-tuple-element.326), channel_id=1, source_target_pairs={{8,0},{16,8},{24,16},{32,24},{40,32},{48,40},{56,48},{64,56},{72,6... | collective-permute-start | bytes 98312 | tf_op jit(solution)/shard_map/ppermute | solution.py:108
  15.3 3.9 %copy-start.16 = (f32[8,1]{0,1:T(1,128)S(1)}, f32[8,1]{0,1:T(1,128)}, u32[]{:S(2)}) copy-start(f32[8,1]{0,1:T(1,128)} %param.13) | copy-start | bytes 100
  15.3 4.0 %copy-start.17 = (f32[8,1]{0,1:T(1,128)S(1)}, f32[8,1]{0,1:T(1,128)}, u32[]{:S(2)}) copy-start(f32[8,1]{0,1:T(1,128)} %param.12) | copy-start | bytes 100
  68.8 54.2 %copy-start = (f32[32,132,128]{2,0,1:T(8,128)}, f32[32,132,128]{2,0,1:T(8,128)S(1)}, u32[]{:S(2)}) copy-start(f32[32,132,128]{2,0,1:T(8,128)S(1)} %pad_maximum_fusion) | copy-start | bytes 6488068
  75.1 9.1 %collective-permute-start.2 = (f32[32,132,2]{1,0,2:T(8,128)S(1)}, f32[32,132,2]{1,0,2:T(8,128)S(1)}, u32[]{:S(2)}, u32[]{:S(2)}) collective-permute-start(f32[32,132,2]{1,0,2:T(8,128)S(1)} %copy.80), channel_id=1, source_target_pairs={{0,1},{1,2},{2,3},{3,4},{4,5},{5,6},{6,7},{8,9},{9,10},{10,11},{11... | collective-permute-start | bytes 101384 | tf_op jit(solution)/shard_map/ppermute | solution.py:116
  80.2 5.5 %collective-permute-start.3 = (f32[32,132,2]{1,0,2:T(8,128)S(1)}, f32[32,132,2]{1,0,2:T(8,128)S(1)}, u32[]{:S(2)}, u32[]{:S(2)}) collective-permute-start(f32[32,132,2]{1,0,2:T(8,128)S(1)} %copy.81), channel_id=1, source_target_pairs={{1,0},{2,1},{3,2},{4,3},{5,4},{6,5},{7,6},{9,8},{10,9},{11,10},{12... | collective-permute-start | bytes 101384 | tf_op jit(solution)/shard_map/ppermute | solution.py:117
  86.2 22.8 %collective-permute-start.4 = (f32[16,84,128]{2,0,1:T(8,128)S(1)}, f32[16,84,128]{2,0,1:T(8,128)S(1)}, u32[]{:S(2)}, u32[]{:S(2)}) collective-permute-start(f32[16,84,128]{2,0,1:T(8,128)S(1)} %constant_dynamic-update-slice_fusion), channel_id=1, source_target_pairs={{0,16},{8,24},{16,32},{24,40},{32,48},{40,56},{48,64},{56,72},{64,... | collective-permute-start | bytes 2064392 | tf_op jit(solution)/shard_map/ppermute | solution.py:28
  89.9 33.1 %collective-permute-start.5 = (f32[16,84,128]{2,0,1:T(8,128)S(1)}, f32[16,84,128]{2,0,1:T(8,128)S(1)}, u32[]{:S(2)}, u32[]{:S(2)}) collective-permute-start(f32[16,84,128]{2,0,1:T(8,128)S(1)} %constant_dynamic-update-slice_fusion.5), channel_id=1, source_target_pairs={{0,8},{8,16},{16,24},{24,32},{32,40},{40,48},{48,56},{56,64},{64,7... | collective-permute-start | bytes 2064392 | tf_op jit(solution)/shard_map/ppermute | solution.py:28
  92.7 71.7 %collective-permute-start.6 = (f32[16,84,128]{2,0,1:T(8,128)S(1)}, f32[16,84,128]{2,0,1:T(8,128)S(1)}, u32[]{:S(2)}, u32[]{:S(2)}) collective-permute-start(f32[16,84,128]{2,0,1:T(8,128)S(1)} %constant_dynamic-update-slice_fusion.10), channel_id=1, source_target_pairs={{8,0},{16,8},{24,16},{32,24},{40,32},{48,40},{56,48},{64,56},{72,6... | collective-permute-start | bytes 2064392 | tf_op jit(solution)/shard_map/ppermute | solution.py:28
  98.1 68.2 %collective-permute-start.7 = (f32[16,84,128]{2,0,1:T(8,128)S(1)}, f32[16,84,128]{2,0,1:T(8,128)S(1)}, u32[]{:S(2)}, u32[]{:S(2)}) collective-permute-start(f32[16,84,128]{2,0,1:T(8,128)S(1)} %constant_dynamic-update-slice_fusion.15), channel_id=1, source_target_pairs={{16,0},{24,8},{32,16},{40,24},{48,32},{56,40},{64,48},{72,56},{80,... | collective-permute-start | bytes 2064392 | tf_op jit(solution)/shard_map/ppermute | solution.py:28
  127.3 118.2 %collective-permute-start.11 = (f32[16,84,128]{2,0,1:T(8,128)}, f32[16,84,128]{2,0,1:T(8,128)}, u32[]{:S(2)}, u32[]{:S(2)}) collective-permute-start(f32[16,84,128]{2,0,1:T(8,128)} %constant_dynamic-update-slice_fusion.52), channel_id=1, source_target_pairs={{16,0},{24,8},{32,16},{40,24},{48,32},{56,40},{64,48},{72,56},{80,... | collective-permute-start | bytes 2064392 | tf_op jit(solution)/shard_map/ppermute | solution.py:28
  130.2 117.5 %collective-permute-start.10 = (f32[16,84,128]{2,0,1:T(8,128)}, f32[16,84,128]{2,0,1:T(8,128)}, u32[]{:S(2)}, u32[]{:S(2)}) collective-permute-start(f32[16,84,128]{2,0,1:T(8,128)} %constant_dynamic-update-slice_fusion.47), channel_id=1, source_target_pairs={{8,0},{16,8},{24,16},{32,24},{40,32},{48,40},{56,48},{64,56},{72,6... | collective-permute-start | bytes 2064392 | tf_op jit(solution)/shard_map/ppermute | solution.py:28
  146.8 102.8 %collective-permute-start.9 = (f32[16,84,128]{2,0,1:T(8,128)}, f32[16,84,128]{2,0,1:T(8,128)}, u32[]{:S(2)}, u32[]{:S(2)}) collective-permute-start(f32[16,84,128]{2,0,1:T(8,128)} %constant_dynamic-update-slice_fusion.42), channel_id=1, source_target_pairs={{0,8},{8,16},{16,24},{24,32},{32,40},{40,48},{48,56},{56,64},{64,7... | collective-permute-start | bytes 2064392 | tf_op jit(solution)/shard_map/ppermute | solution.py:28
  164.4 87.2 %collective-permute-start.8 = (f32[16,84,128]{2,0,1:T(8,128)}, f32[16,84,128]{2,0,1:T(8,128)}, u32[]{:S(2)}, u32[]{:S(2)}) collective-permute-start(f32[16,84,128]{2,0,1:T(8,128)} %constant_dynamic-update-slice_fusion.37), channel_id=1, source_target_pairs={{0,16},{8,24},{16,32},{24,40},{32,48},{40,56},{48,64},{56,72},{64,... | collective-permute-start | bytes 2064392 | tf_op jit(solution)/shard_map/ppermute | solution.py:28
  166.4 1.8 copy-start.11
  175.4 2.1 copy-start.9
  179.6 3.2 %copy-start.3 = (f32[8,8,16,128]{3,1,2,0:T(8,128)S(1)}, f32[8,8,16,128]{3,1,2,0:T(8,128)}, u32[]{:S(2)}) copy-start(f32[8,8,16,128]{3,1,2,0:T(8,128)} %get-tuple-element.402) | copy-start | bytes 1572868
  193.5 57.2 %copy-start.5 = (f32[2,8,128,128]{3,2,0,1:T(8,128)}, f32[2,8,128,128]{3,2,0,1:T(8,128)S(1)}, u32[]{:S(2)}) copy-start(f32[2,8,128,128]{3,2,0,1:T(8,128)S(1)} %convolution_bitcast_fusion) | copy-start | bytes 3145732
  245.6 8.0 %copy-start.7 = (f32[160,8,128]{2,1,0:T(8,128)}, f32[160,8,128]{2,1,0:T(8,128)S(1)}, u32[]{:S(2)}) copy-start(f32[160,8,128]{2,1,0:T(8,128)S(1)} %all-gather) | copy-start | bytes 1966084
  251.5 2.2 copy-start.1
  254.2 2.9 %copy-start.10 = (f32[8,16,20,128]{3,1,2,0:T(8,128)}, f32[8,16,20,128]{3,1,2,0:T(8,128)S(1)}, u32[]{:S(2)}) copy-start(f32[8,16,20,128]{3,1,2,0:T(8,128)S(1)} %constant_dynamic-update-slice_fusion.134) | copy-start | bytes 3932164
  270.3 11.2 %copy-start.8 = (f32[160,8,128]{2,1,0:T(8,128)S(1)}, f32[160,8,128]{2,1,0:T(8,128)}, u32[]{:S(2)}) copy-start(f32[160,8,128]{2,1,0:T(8,128)} %copy-done.7) | copy-start | bytes 1966084
  270.3 11.2 %copy-start.15 = (f32[32,2,8,128]{3,2,1,0:T(8,128)S(1)}, f32[32,2,8,128]{3,2,1,0:T(8,128)}, u32[]{:S(2)}) copy-start(f32[32,2,8,128]{3,2,1,0:T(8,128)} %constant_dynamic-update-slice_fusion.88) | copy-start | bytes 786436
  272.9 11.8 %copy-start.6 = (f32[2,8,128,128]{3,2,0,1:T(8,128)S(1)}, f32[2,8,128,128]{3,2,0,1:T(8,128)}, u32[]{:S(2)}) copy-start(f32[2,8,128,128]{3,2,0,1:T(8,128)} %copy-done.5) | copy-start | bytes 3145732
